TPU v7x, 1024 devices: a whole 4x8x16 slice. The times are simulated.
1024 devices in a mesh: dp: 16 (over y, z_hi), gz: 64 (over x, z_lo, core).
Axes of the slice: x: 4, y: 8, z: 16 (z_hi: 2, z_lo: 8; z = z_hi * 8 + z_lo), core: 2. Of those that a mesh axis runs over, the one named last changes fastest.
Arguments:
- volume: bfloat16 [64, 16, 16, 2048], P('gz', 'dp'), may hold values from -6 to 6
- weight: bfloat16 [1728, 64], replicated, may hold values from -0.15625 to 0.15625
- cotangent: bfloat16 [64, 16, 16, 2048], P('gz', 'dp'), may hold values from -6 to 6
Outputs:
- activation: bfloat16 [64, 16, 16, 2048], P('gz', 'dp')
- input_grad: bfloat16 [64, 16, 16, 2048], P('gz', 'dp')
- weight_grad: float32 [1728, 64], P('gz', 'dp')
All inputs are finite; a program needn't handle non-finite values.
Results may differ from a plain program's by a relative error of at most 0.01.
Values may be sent and summed in bfloat16 or wider, within the bound.
No kernel may reach another device: no remote copies, remote signals or barrier semaphores. Data moves between devices by JAX's collectives and lax.ppermute only.
A program may use at most 32 MiB of HBM per device.

v0:
```python
import math

import jax
import jax.numpy as jnp
from jax import lax
from jax.sharding import PartitionSpec as P


def padded_2(block, sides, width):
    for axis, dim in sides:
        count = lax.axis_size(axis)
        forward = [(i, i + 1) for i in range(count - 1)]
        backward = [(target, source) for source, target in forward]
        low = lax.ppermute(
            lax.slice_in_dim(block, block.shape[dim] - width, None, axis=dim), axis, forward
        )
        high = lax.ppermute(lax.slice_in_dim(block, 0, width, axis=dim), axis, backward)
        block = jnp.concatenate([low, block, high], axis=dim)
    return block


def split_up(value, dim, size):
    dims = value.shape
    pieces = value.reshape(*dims[:dim], size, dims[dim] // size, *dims[dim + 1 :])
    return jnp.moveaxis(pieces, dim, 0)


def sum_at_owner(value, axis, dim):
    size = lax.axis_size(axis)
    pieces = lax.all_to_all(split_up(value, dim, size), axis, 0, 0, tiled=True)
    return jnp.sum(pieces.astype(jnp.float32), axis=0)


def sum_at_owner_2(value, axis, dim):
    pieces = split_up(value, dim, lax.axis_size(axis))
    arrived = lax.all_to_all(pieces, axis, split_axis=0, concat_axis=0, tiled=True)
    return arrived.sum(axis=0)


def strips(padded, z_start, y_start, planes, height, width, order):
    parts = [
        padded[z_start : z_start + planes, y_start : y_start + height, x_start : x_start + width]
        for x_start in order
    ]
    joined = jnp.concatenate(parts, axis=-1)
    return joined.reshape(planes * height * width, joined.shape[-1])


def per_device(volume, weight, cotangent):
    chans = weight.shape[1]
    planes = volume.shape[1]
    height = volume.shape[2]
    width = volume.shape[3] // chans
    cells = planes * height * width
    extended = padded_2(volume, (("dp", 1),), 1)
    padded = jnp.pad(
        extended.reshape(planes + 2, height, width, chans), ((0, 0), (1, 1), (1, 1), (0, 0))
    )
    blocks = []
    flipped = []
    for tap_z in range(3):
        for tap_y in range(3):
            first = (tap_z * 3 + tap_y) * 3 * chans
            block = weight[first : first + 3 * chans]
            blocks.append(block)
            flipped.append(
                block.reshape(3, chans, chans).transpose(0, 2, 1).reshape(3 * chans, chans)
            )
    pre = jnp.zeros((cells, chans), jnp.float32)
    for tap_z in range(3):
        for tap_y in range(3):
            window = strips(padded, tap_z, tap_y, planes, height, width, (0, 1, 2))
            pre = pre + jnp.dot(
                window, blocks[tap_z * 3 + tap_y], preferred_element_type=jnp.float32
            )
    sig = jax.nn.sigmoid(pre)
    activation = (pre * sig).astype(jnp.bfloat16).reshape(1, planes, height, width * chans)
    delta = (
        cotangent.reshape(cells, chans).astype(jnp.float32) * sig * (1.0 + pre * (1.0 - sig))
    ).astype(jnp.bfloat16)
    delta_ext = padded_2(delta.reshape(1, planes, height, width * chans), (("dp", 1),), 1)
    delta_pad = jnp.pad(
        delta_ext.reshape(planes + 2, height, width, chans), ((0, 0), (1, 1), (1, 1), (0, 0))
    )
    back = jnp.zeros((cells, chans), jnp.float32)
    for tap_z in range(3):
        for tap_y in range(3):
            window = strips(delta_pad, 2 - tap_z, 2 - tap_y, planes, height, width, (2, 1, 0))
            back = back + jnp.dot(
                window, flipped[tap_z * 3 + tap_y], preferred_element_type=jnp.float32
            )
    summed = back.reshape(planes, height, width * chans)
    input_grad = summed.astype(jnp.bfloat16).reshape(1, planes, height, width * chans)
    pieces = []
    for tap_z in range(3):
        for tap_y in range(3):
            window = strips(padded, tap_z, tap_y, planes, height, width, (0, 1, 2))
            pieces.append(
                lax.dot_general(
                    window, delta, (((0,), (0,)), ((), ())), preferred_element_type=jnp.float32
                )
            )
    scale = 1.0 / math.sqrt(lax.axis_size("dp") * lax.axis_size("gz") * cells)
    terms = jnp.concatenate(pieces, axis=0) * scale
    reduced = sum_at_owner(terms.astype(jnp.bfloat16), "dp", 1)
    weight_grad = sum_at_owner_2(reduced, "gz", 0)
    return (activation, input_grad, weight_grad)


def solution(mesh):
    return jax.shard_map(
        per_device,
        mesh=mesh,
        in_specs=(P("gz", "dp", None, None), P(), P("gz", "dp", None, None)),
        out_specs=(P("gz", "dp", None, None), P("gz", "dp", None, None), P("gz", "dp")),
        check_vma=False,
    )
```

profile of v0, /device:TPU:1, one launch (start us, length us, event | category | flops | bytes accessed | tf_op | source)
XLA Modules:
  0.0 130.6 jit_solution(14968479860423085455)
XLA Ops:
  0.6 20.0 %collective-permute-start = (bf16[1,1,16,2048]{3,2,1,0:T(8,128)(2,1)}, bf16[1,1,16,2048]{3,2,1,0:T(8,128)(2,1)S(1)}, u32[]{:S(2)}, u32[]{:S(2)}) collective-permute-start(bf16[1,1,16,2048]{3,2,1,0:T(8,128)(2,1)} %param.3), channel_id=1, source_target_pairs={{0,64},{64,128},{128,192},{192,256},{256,320},{320,384},{384,448},... | collective-permute-start | bytes 196616 | tf_op jit(solution)/shard_map/ppermute | solution.py:14
  20.7 1.3 collective-permute-start.1
  22.0 1.0 fusion.75
  23.5 0.8 copy.84
  24.4 0.7 copy.87
  25.2 0.7 copy.88
  26.1 0.7 copy.89
  26.9 0.7 copy.90
  27.7 0.7 copy.93
  28.5 0.7 copy.94
  29.4 0.7 copy.95
  30.2 0.7 copy.96
  31.0 0.7 copy.97
  31.7 5.7 %collective-permute-done.1 = bf16[1,1,16,2048]{3,2,1,0:T(8,128)(2,1)S(1)} collective-permute-done((bf16[1,1,16,2048]{3,2,1,0:T(8,128)(2,1)}, bf16[1,1,16,2048]{3,2,1,0:T(8,128)(2,1)S(1)}, u32[]{:S(2)}, u32[]{:S(2)}) %collective-permute-start.1) | collective-permute-done | bytes 65568 | tf_op jit(solution)/shard_map/ppermute | solution.py:17
  37.4 0.6 copy-done.6
  38.1 0.4 reshape.193
  38.5 0.5 pad_slice_fusion.4
  39.0 0.8 pad_slice_fusion.3
  40.0 0.7 copy-done
  40.7 0.9 fusion.66
  41.5 0.9 fusion.68
  42.4 0.3 pad_maximum_fusion
  42.7 0.8 fusion.71
  45.1 0.7 copy.78
  45.9 0.7 copy.80
  46.8 0.7 copy.79
  48.0 0.7 copy-done.16
  48.7 0.3 multiply_convert_fusion.1
  49.9 7.0 %collective-permute-start.2 = (bf16[1,1,16,2048]{3,2,1,0:T(8,128)(2,1)S(1)}, bf16[1,1,16,2048]{3,2,1,0:T(8,128)(2,1)S(1)}, u32[]{:S(2)}, u32[]{:S(2)}) collective-permute-start(bf16[1,1,16,2048]{3,2,1,0:T(8,128)(2,1)S(1)} %reshape.201), channel_id=1, source_target_pairs={{0,64},{64,128},{128,192},{192,256},{256,320},{320,384},{384,448},... | collective-permute-start | bytes 196616 | tf_op jit(solution)/shard_map/ppermute | solution.py:14
  56.9 1.3 collective-permute-start.3
  59.5 0.8 copy.114
  60.3 17.4 %all-to-all-start = ((bf16[16,1728,4]{1,2,0:T(4,128)(2,1)}), bf16[16,1728,4]{1,2,0:T(4,128)(2,1)S(1)}, u32[]{:S(2)}, u32[]{:S(2)}) async-start(bf16[16,1728,4]{1,2,0:T(4,128)(2,1)} %copy.114), calls=%async_computation | async-start | bytes 458752 | tf_op jit(solution)/shard_map/all_to_all | solution.py:30
  77.9 0.8 reshape.200
  79.3 0.4 fusion.73
  79.7 0.8 fusion.74
  80.8 0.4 copy-done.14
  82.1 0.5 copy-done.17
  82.7 0.3 convolution_add_fusion.10
  83.2 0.3 copy-done.13
  84.5 0.4 copy-done.10
  85.4 0.4 copy-done.22
  85.8 0.3 convolution_add_fusion.4
  86.1 9.0 %all-to-all-done = bf16[16,1728,4]{1,2,0:T(4,128)(2,1)S(1)} async-done(((bf16[16,1728,4]{1,2,0:T(4,128)(2,1)}), bf16[16,1728,4]{1,2,0:T(4,128)(2,1)S(1)}, u32[]{:S(2)}, u32[]{:S(2)}) %all-to-all-start) | async-done | bytes 221216 | tf_op jit(solution)/shard_map/all_to_all | solution.py:30
  95.3 0.7 copy.115
  96.0 19.3 %all-to-all-start.1 = ((f32[64,27,4]{1,2,0:T(4,128)}), f32[64,27,4]{1,2,0:T(4,128)S(1)}, u32[]{:S(2)}, u32[]{:S(2)}) async-start(f32[64,27,4]{1,2,0:T(4,128)} %copy.115), calls=%async_computation.1 | async-start | bytes 262144 | tf_op jit(solution)/shard_map/all_to_all | solution.py:36
  115.7 0.8 convert_element_type.42
  116.5 13.4 %all-to-all-done.1 = f32[64,27,4]{1,2,0:T(4,128)S(1)} async-done(((f32[64,27,4]{1,2,0:T(4,128)}), f32[64,27,4]{1,2,0:T(4,128)S(1)}, u32[]{:S(2)}, u32[]{:S(2)}) %all-to-all-start.1) | async-done | bytes 27680 | tf_op jit(solution)/shard_map/all_to_all | solution.py:36
  129.9 0.7 reduce_sum.19
  (110 shorter events, 10.0 us)
Async XLA Ops:
  0.6 22.4 %copy-start.5 = (bf16[1,1,16,2048]{3,2,1,0:T(8,128)(2,1)S(1)}, bf16[1,1,16,2048]{3,2,1,0:T(8,128)(2,1)}, u32[]{:S(2)}) copy-start(bf16[1,1,16,2048]{3,2,1,0:T(8,128)(2,1)} %param.3) | copy-start | bytes 196612
  0.6 22.7 %copy-start.18 = (bf16[1,1,16,2048]{3,2,1,0:T(8,128)(2,1)S(1)}, bf16[1,1,16,2048]{3,2,1,0:T(8,128)(2,1)}, u32[]{:S(2)}) copy-start(bf16[1,1,16,2048]{3,2,1,0:T(8,128)(2,1)} %param.5) | copy-start | bytes 196612
  0.6 31.1 %collective-permute-start = (bf16[1,1,16,2048]{3,2,1,0:T(8,128)(2,1)}, bf16[1,1,16,2048]{3,2,1,0:T(8,128)(2,1)S(1)}, u32[]{:S(2)}, u32[]{:S(2)}) collective-permute-start(bf16[1,1,16,2048]{3,2,1,0:T(8,128)(2,1)} %param.3), channel_id=1, source_target_pairs={{0,64},{64,128},{128,192},{192,256},{256,320},{320,384},{384,448},... | collective-permute-start | bytes 196616 | tf_op jit(solution)/shard_map/ppermute | solution.py:14
  20.7 16.7 %collective-permute-start.1 = (bf16[1,1,16,2048]{3,2,1,0:T(8,128)(2,1)}, bf16[1,1,16,2048]{3,2,1,0:T(8,128)(2,1)S(1)}, u32[]{:S(2)}, u32[]{:S(2)}) collective-permute-start(bf16[1,1,16,2048]{3,2,1,0:T(8,128)(2,1)} %param.3), channel_id=1, source_target_pairs={{64,0},{128,64},{192,128},{256,192},{320,256},{384,320},{448,384},... | collective-permute-start | bytes 196616 | tf_op jit(solution)/shard_map/ppermute | solution.py:17
  31.7 7.2 %copy-start.8 = (bf16[1,1,16,2048]{3,2,1,0:T(8,128)(2,1)}, bf16[1,1,16,2048]{3,2,1,0:T(8,128)(2,1)S(1)}, u32[]{:S(2)}) copy-start(bf16[1,1,16,2048]{3,2,1,0:T(8,128)(2,1)S(1)} %collective-permute-done) | copy-start | bytes 196612
  37.4 0.6 copy-start.6
  39.7 0.9 copy-start
  42.7 1.1 copy-start.9
  44.7 1.2 copy-start.4
  44.8 1.8 %copy-start.7 = (bf16[1,1,16,2048]{3,2,1,0:T(8,128)(2,1)S(1)}, bf16[1,1,16,2048]{3,2,1,0:T(8,128)(2,1)}, u32[]{:S(2)}) copy-start(bf16[1,1,16,2048]{3,2,1,0:T(8,128)(2,1)} %copy-done.6) | copy-start | bytes 196612
  44.9 2.6 %copy-start.1 = (f32[512,64]{0,1:T(8,128)S(1)}, f32[512,64]{0,1:T(8,128)}, u32[]{:S(2)}) copy-start(f32[512,64]{0,1:T(8,128)} %fusion.66) | copy-start | bytes 393220
  44.9 2.6 %copy-start.2 = (f32[512,64]{0,1:T(8,128)S(1)}, f32[512,64]{0,1:T(8,128)}, u32[]{:S(2)}) copy-start(f32[512,64]{0,1:T(8,128)} %fusion.68) | copy-start | bytes 393220
  44.9 2.6 %copy-start.3 = (f32[512,64]{0,1:T(8,128)S(1)}, f32[512,64]{0,1:T(8,128)}, u32[]{:S(2)}) copy-start(f32[512,64]{0,1:T(8,128)} %fusion.71) | copy-start | bytes 393220
  47.7 0.9 copy-start.16
  47.8 0.9 copy-start.19
  47.8 0.9 copy-start.20
  47.8 0.9 copy-start.21
  49.9 28.8 %collective-permute-start.2 = (bf16[1,1,16,2048]{3,2,1,0:T(8,128)(2,1)S(1)}, bf16[1,1,16,2048]{3,2,1,0:T(8,128)(2,1)S(1)}, u32[]{:S(2)}, u32[]{:S(2)}) collective-permute-start(bf16[1,1,16,2048]{3,2,1,0:T(8,128)(2,1)S(1)} %reshape.201), channel_id=1, source_target_pairs={{0,64},{64,128},{128,192},{192,256},{256,320},{320,384},{384,448},... | collective-permute-start | bytes 196616 | tf_op jit(solution)/shard_map/ppermute | solution.py:14
  56.9 22.0 %collective-permute-start.3 = (bf16[1,1,16,2048]{3,2,1,0:T(8,128)(2,1)S(1)}, bf16[1,1,16,2048]{3,2,1,0:T(8,128)(2,1)S(1)}, u32[]{:S(2)}, u32[]{:S(2)}) collective-permute-start(bf16[1,1,16,2048]{3,2,1,0:T(8,128)(2,1)S(1)} %reshape.201), channel_id=1, source_target_pairs={{64,0},{128,64},{192,128},{256,192},{320,256},{384,320},{448,384},... | collective-permute-start | bytes 196616 | tf_op jit(solution)/shard_map/ppermute | solution.py:17
  60.3 34.7 %all-to-all-start = ((bf16[16,1728,4]{1,2,0:T(4,128)(2,1)}), bf16[16,1728,4]{1,2,0:T(4,128)(2,1)S(1)}, u32[]{:S(2)}, u32[]{:S(2)}) async-start(bf16[16,1728,4]{1,2,0:T(4,128)(2,1)} %copy.114), calls=%async_computation | async-start | bytes 458752 | tf_op jit(solution)/shard_map/all_to_all | solution.py:30
  80.4 0.8 copy-start.14
  81.8 0.9 copy-start.17
  81.8 0.9 copy-start.24
  81.9 1.0 copy-start.12
  82.7 0.8 copy-start.13
  83.0 0.8 copy-start.23
  84.2 0.8 copy-start.10
  84.3 0.8 copy-start.11
  85.0 0.8 copy-start.22
  86.1 29.3 %copy-start.15 = (bf16[3,64,64]{2,1,0:T(8,128)(2,1)S(1)}, bf16[3,64,64]{2,1,0:T(8,128)(2,1)}, u32[]{:S(2)}) copy-start(bf16[3,64,64]{2,1,0:T(8,128)(2,1)} %copy.97) | copy-start | bytes 73732
  96.0 33.9 %all-to-all-start.1 = ((f32[64,27,4]{1,2,0:T(4,128)}), f32[64,27,4]{1,2,0:T(4,128)S(1)}, u32[]{:S(2)}, u32[]{:S(2)}) async-start(f32[64,27,4]{1,2,0:T(4,128)} %copy.115), calls=%async_computation.1 | async-start | bytes 262144 | tf_op jit(solution)/shard_map/all_to_all | solution.py:36
where the time goes:
time: 131 us
  starting transfers between devices  66.4 us (51%)
  waiting for transfers between devices  28.1 us (21%)
  local copies, waits for them, and re-layouts  24.8 us (19%)
  matrix products  7.41 us (6%)
  other arithmetic  2.66 us (2%)
    ppermute x2, starting transfers between devices, padded_2(): lax.ppermute(lax.slice_in_dim(block, block.shape[dim] - width, None, axis...  27.1 us
    all_to_all x1, starting transfers between devices, sum_at_owner_2(): lax.all_to_all(pieces, axis, split_axis=0, concat_axis=0, tiled=True)  19.3 us
    all_to_all x1, starting transfers between devices, sum_at_owner(): pieces = lax.all_to_all(split_up(value, dim, size), axis, 0, 0, tiled=True)  17.4 us
    all_to_all x1, waiting for transfers between devices, sum_at_owner_2(): lax.all_to_all(pieces, axis, split_axis=0, concat_axis=0, tiled=True)  13.4 us
    all_to_all x1, waiting for transfers between devices, sum_at_owner(): pieces = lax.all_to_all(split_up(value, dim, size), axis, 0, 0, tiled=True)  8.98 us
    transpose x9, local copies, waits for them, and re-layouts, per_device(): block.reshape(3, chans, chans).transpose(0, 2, 1).reshape(3 * chans, chans)  6.47 us
    unnamed x60, local copies, waits for them, and re-layouts  6.33 us
    ppermute x2, waiting for transfers between devices, padded_2(): lax.ppermute(lax.slice_in_dim(block, 0, width, axis=dim), axis, backward)  5.69 us
  transfers between devices with their start and end apart: 6, of which 3 were waited for; matrix products, arithmetic and copies ran while one was open for 14% of the time, Pallas kernels for 0%

commit v1 on v0

--- a/solution.py
+++ b/solution.py
@@ -46,15 +46,36 @@
     return joined.reshape(planes * height * width, joined.shape[-1])
 
 
+def halo_planes(block, axis, depth):
+    count = lax.axis_size(axis)
+    planes = block.shape[1]
+    below, above = [], []
+    for shift in range(1, -(-depth // planes) + 1):
+        forward = [(i, i + shift) for i in range(count - shift)]
+        backward = [(target, source) for source, target in forward]
+        below.insert(0, lax.ppermute(block, axis, forward))
+        above.append(lax.ppermute(block, axis, backward))
+    low = jnp.concatenate(below, axis=1)
+    high = jnp.concatenate(above, axis=1)
+    low = lax.slice_in_dim(low, low.shape[1] - depth, None, axis=1)
+    high = lax.slice_in_dim(high, 0, depth, axis=1)
+    return low, high
+
+
 def per_device(volume, weight, cotangent):
     chans = weight.shape[1]
     planes = volume.shape[1]
     height = volume.shape[2]
     width = volume.shape[3] // chans
     cells = planes * height * width
-    extended = padded_2(volume, (("dp", 1),), 1)
+    both = jnp.concatenate([volume, cotangent], axis=0)
+    low1, high1 = halo_planes(both, "dp", 1)
+    low2, high2 = halo_planes(volume, "dp", 2)
+    v_ext = jnp.concatenate([low2[:, :1], low1[:1], volume, high1[:1], high2[:, 1:]], axis=1)
+    c_ext = jnp.concatenate([low1[1:], cotangent, high1[1:]], axis=1)
+    ext = planes + 2
     padded = jnp.pad(
-        extended.reshape(planes + 2, height, width, chans), ((0, 0), (1, 1), (1, 1), (0, 0))
+        v_ext.reshape(planes + 4, height, width, chans), ((0, 0), (1, 1), (1, 1), (0, 0))
     )
     blocks = []
     flipped = []
@@ -66,21 +87,25 @@
             flipped.append(
                 block.reshape(3, chans, chans).transpose(0, 2, 1).reshape(3 * chans, chans)
             )
-    pre = jnp.zeros((cells, chans), jnp.float32)
+    pre = jnp.zeros((ext * height * width, chans), jnp.float32)
     for tap_z in range(3):
         for tap_y in range(3):
-            window = strips(padded, tap_z, tap_y, planes, height, width, (0, 1, 2))
+            window = strips(padded, tap_z, tap_y, ext, height, width, (0, 1, 2))
             pre = pre + jnp.dot(
                 window, blocks[tap_z * 3 + tap_y], preferred_element_type=jnp.float32
             )
     sig = jax.nn.sigmoid(pre)
-    activation = (pre * sig).astype(jnp.bfloat16).reshape(1, planes, height, width * chans)
-    delta = (
-        cotangent.reshape(cells, chans).astype(jnp.float32) * sig * (1.0 + pre * (1.0 - sig))
+    inner = slice(height * width, (planes + 1) * height * width)
+    activation = (pre[inner] * sig[inner]).astype(jnp.bfloat16)
+    activation = activation.reshape(1, planes, height, width * chans)
+    delta_ext = (
+        c_ext.reshape(ext * height * width, chans).astype(jnp.float32)
+        * sig
+        * (1.0 + pre * (1.0 - sig))
     ).astype(jnp.bfloat16)
-    delta_ext = padded_2(delta.reshape(1, planes, height, width * chans), (("dp", 1),), 1)
+    delta = delta_ext[inner]
     delta_pad = jnp.pad(
-        delta_ext.reshape(planes + 2, height, width, chans), ((0, 0), (1, 1), (1, 1), (0, 0))
+        delta_ext.reshape(ext, height, width, chans), ((0, 0), (1, 1), (1, 1), (0, 0))
     )
     back = jnp.zeros((cells, chans), jnp.float32)
     for tap_z in range(3):
@@ -94,7 +119,7 @@
     pieces = []
     for tap_z in range(3):
         for tap_y in range(3):
-            window = strips(padded, tap_z, tap_y, planes, height, width, (0, 1, 2))
+            window = strips(padded, 1 + tap_z, tap_y, planes, height, width, (0, 1, 2))
             pieces.append(
                 lax.dot_general(
                     window, delta, (((0,), (0,)), ((), ())), preferred_element_type=jnp.float32

time: 131 us -> 163 us (1.24)
  local copies, waits for them, and re-layouts: 24.8 us -> 48.7 us
  starting transfers between devices: 66.4 us -> 56.8 us
  matrix products: 7.41 us -> 14.3 us
  other arithmetic: 2.66 us -> 8.36 us
  waiting for transfers between devices: 28.1 us -> 32.2 us
    slice x4 -> x6, local copies, waits for them, and re-layouts: 2.44 us -> 10.7 us  [strips(): padded[z_start:z_start + planes, y_start:y_start + height, x_start:x_star...]
    concatenate x16 -> x21, local copies, waits for them, and re-layouts: 3.85 us -> 11.7 us  [strips(): joined = jnp.concatenate(parts, axis=-1)]
    all_to_all x1, starting transfers between devices: 19.3 us -> 14.9 us  [sum_at_owner_2(): lax.all_to_all(pieces, axis, split_axis=0, concat_axis=0, tiled=True)]
    dot_general x9, matrix products: 1.6 us -> 5.81 us  [per_device(): lax.dot_general(window, delta, (((0,), (0,)), ((), ())), preferred_elemen...]
    concatenate x9 -> x12, other arithmetic: 1.65 us -> 5.59 us  [strips(): joined = jnp.concatenate(parts, axis=-1)]
    ppermute x4, starting transfers between devices: 29.7 us -> 25.8 us  [the longest x2 23.2 us: halo_planes(): below.insert(0, lax.ppermute(block, axis, forward))]
    ppermute x4, waiting for transfers between devices: 5.69 us -> 9.53 us  [the longest x2 9.52 us: halo_planes(): above.append(lax.ppermute(block, axis, backward))]
    unnamed x60 -> x183, local copies, waits for them, and re-layouts: 6.33 us -> 9.35 us
  transfers between devices with their start and end apart: 6 -> 6, of which waited for: 3 -> 3; matrix products, arithmetic and copies ran while one was open for 14% -> 12% of each run, Pallas kernels for 0% -> 0%
where the time goes in v1:
time: 163 us; the launch traced here: 162 us
  starting transfers between devices  56.8 us (35%)
  local copies, waits for them, and re-layouts  48.7 us (30%)
  waiting for transfers between devices  32.2 us (20%)
  matrix products  14.3 us (9%)
  other arithmetic  8.36 us (5%)
  between operations  1.73 us (1%)
    ppermute x2, starting transfers between devices, halo_planes(): below.insert(0, lax.ppermute(block, axis, forward))  23.2 us
    all_to_all x1, starting transfers between devices, sum_at_owner(): pieces = lax.all_to_all(split_up(value, dim, size), axis, 0, 0, tiled=True)  16 us
    all_to_all x1, starting transfers between devices, sum_at_owner_2(): lax.all_to_all(pieces, axis, split_axis=0, concat_axis=0, tiled=True)  14.9 us
    all_to_all x1, waiting for transfers between devices, sum_at_owner_2(): lax.all_to_all(pieces, axis, split_axis=0, concat_axis=0, tiled=True)  12.6 us
    concatenate x21, local copies, waits for them, and re-layouts, strips(): joined = jnp.concatenate(parts, axis=-1)  11.7 us
    slice x6, local copies, waits for them, and re-layouts, strips(): padded[z_start:z_start + planes, y_start:y_start + height, x_start:x_star...  10.7 us
    all_to_all x1, waiting for transfers between devices, sum_at_owner(): pieces = lax.all_to_all(split_up(value, dim, size), axis, 0, 0, tiled=True)  10 us
    ppermute x2, waiting for transfers between devices, halo_planes(): above.append(lax.ppermute(block, axis, backward))  9.52 us
  transfers between devices with their start and end apart: 6, of which 3 were waited for; matrix products, arithmetic and copies ran while one was open for 12% of the time, Pallas kernels for 0%

profile of v1, /device:TPU:1, one launch (start us, length us, event | category | flops | bytes accessed | tf_op | source)
XLA Modules:
  0.0 162.0 jit_solution(15735857882699701531)
XLA Ops:
  0.6 4.2 %collective-permute-start = (bf16[1,1,16,2048]{3,2,1,0:T(8,128)(2,1)}, bf16[1,1,16,2048]{3,2,1,0:T(8,128)(2,1)S(1)}, u32[]{:S(2)}, u32[]{:S(2)}) collective-permute-start(bf16[1,1,16,2048]{3,2,1,0:T(8,128)(2,1)} %param.3), channel_id=1, source_target_pairs={{0,128},{64,192},{128,256},{192,320},{256,384},{320,448},{384,512}... | collective-permute-start | bytes 196616 | tf_op jit(solution)/shard_map/ppermute | solution.py:56
  4.8 0.9 constant_dynamic-update-slice_fusion.1
  5.7 0.8 constant_dynamic-update-slice_fusion
  6.5 19.1 %collective-permute-start.1 = (bf16[2,1,16,2048]{3,2,1,0:T(8,128)(2,1)S(1)}, bf16[2,1,16,2048]{3,2,1,0:T(8,128)(2,1)S(1)}, u32[]{:S(2)}, u32[]{:S(2)}) collective-permute-start(bf16[2,1,16,2048]{3,2,1,0:T(8,128)(2,1)S(1)} %constant_dynamic-update-slice_fusion), channel_id=1, source_target_pairs={{0,64},{64,128},{128,192},{192,256},{256,320},{320,384},{384,448},... | collective-permute-start | bytes 393224 | tf_op jit(solution)/shard_map/ppermute | solution.py:56
  25.6 1.3 collective-permute-start.2
  26.9 1.3 collective-permute-start.3
  28.2 1.0 fusion.82
  29.4 0.7 copy.108
  31.1 0.7 copy.84
  34.4 0.7 copy.90
  38.3 9.5 %collective-permute-done.2 = bf16[2,1,16,2048]{3,2,1,0:T(8,128)(2,1)S(1)} collective-permute-done((bf16[2,1,16,2048]{3,2,1,0:T(8,128)(2,1)S(1)}, bf16[2,1,16,2048]{3,2,1,0:T(8,128)(2,1)S(1)}, u32[]{:S(2)}, u32[]{:S(2)}) %collective-permute-start.2) | collective-permute-done | bytes 131104 | tf_op jit(solution)/shard_map/ppermute | solution.py:57
  49.2 4.3 %pad_slice_fusion.26 = (bf16[3,16,32,64]{3,2,1,0:T(8,128)(2,1)S(1)}, bf16[3,16,32,64]{3,2,1,0:T(8,128)(2,1)S(1)}, bf16[3,16,32,64]{3,2,1,0:T(8,128)(2,1)S(1)}, b...) fusion(bf16[5,16,32,64]{3,2,1,0:T(8,128)(2,1)S(1)} %reshape.218), kind=kLoop, calls=%fused_computation.34 | loop fusion | bytes 4063232 | tf_op jit(solution)/shard_map/slice | solution.py:42
  53.5 1.5 pad_slice_fusion.25
  55.0 1.7 %pad_slice_fusion.2 = (bf16[1,16,32,64]{3,2,1,0:T(8,128)(2,1)}, bf16[1,16,32,64]{3,2,1,0:T(8,128)(2,1)}, bf16[1,16,32,64]{3,2,1,0:T(8,128)(2,1)}, bf16[1,16,32,6...) fusion(bf16[5,16,32,64]{3,2,1,0:T(8,128)(2,1)S(1)} %reshape.218), kind=kLoop, calls=%fused_computation.10 | loop fusion | bytes 1572864 | tf_op jit(solution)/shard_map/slice | solution.py:42
  56.6 0.9 pad_slice_fusion.1
  57.5 0.8 pad_maximum_fusion
  58.3 1.9 %fusion.80 = f32[1536,64]{0,1:T(8,128)} fusion(bf16[1536,192]{1,0:T(8,128)(2,1)S(1)} %bitcast.150, bf16[1728,64]{0,1:T(8,128)(2,1)} %param.4), kind=kOutput, calls=%fused_computation.205 | convolution fusion | flops 37748736 | bytes 1015808 | tf_op jit(solution)/shard_map/dot_general | solution.py:94
  60.2 0.8 concatenate.201
  61.0 0.8 concatenate.213
  61.9 1.8 %pad_maximum_fusion.20 = (bf16[1,3,16,2048]{3,2,1,0:T(8,128)(2,1)S(1)}, bf16[1,3,16,2048]{3,2,1,0:T(8,128)(2,1)S(1)}, bf16[1,3,16,2048]{3,2,1,0:T(8,128)(2,1)S(1)}, f32[1,3,16,2048]{3,2,1,0:T(8,128)}) fusion(bf16[1,1,16,2048]{3,2,1,0:T(8,128)(2,1)} %copy-done.56, bf16[1,1,16,2048]{3,2,1,0:T(8,128)(2,1)S(1)} %get-tuple-element.95, ...), kind=kLoop, calls=%fused_computation.129 | loop fusion | flops 884736 | bytes 1507328 | tf_op jit(solution)/shard_map/concatenate | solution.py:74
  63.7 1.2 concatenate.165
  64.8 1.1 concatenate.172
  66.0 1.1 concatenate.179
  67.1 1.3 reshape.258
  68.4 1.0 copy.79
  69.4 2.0 %convolution_add_fusion.7 = f32[1536,64]{0,1:T(8,128)S(1)} fusion(f32[1536,64]{0,1:T(8,128)} %fusion.80, bf16[1536,64]{1,0:T(8,128)(2,1)} %bitcast.172, bf16[1536,64]{1,0:T(8,128)(2,1)} %concatenate.165, bf16[1536,64]{1,0:T(8,128)(2,1)} %bitcast.171, bf16[1728,64]{0,1:T(8,128)(2,1)} %param.4), kind=kOutput, calls=%fused_computation.7 | convolution fusion | flops 39616512 | bytes 1998848 | tf_op jit(solution)/shard_map/dot_general | solution.py:94
  72.7 0.8 pad_maximum_fusion.2
  76.4 0.8 pad_maximum_fusion.4
  81.0 1.4 pad_slice_fusion.50
  82.5 0.9 pad_slice_fusion.49
  85.9 0.8 fusion.53
  86.7 0.8 fusion.56
  89.0 0.9 pad_maximum_fusion.12
  90.0 0.8 fusion.58
  93.0 0.8 fusion.61
  94.2 1.1 fusion.37
  95.3 1.0 fusion.32
  96.8 0.8 copy.121
  97.6 16.0 %all-to-all-start = ((bf16[16,1728,4]{1,2,0:T(4,128)(2,1)}), bf16[16,1728,4]{1,2,0:T(4,128)(2,1)S(1)}, u32[]{:S(2)}, u32[]{:S(2)}) async-start(bf16[16,1728,4]{1,2,0:T(4,128)(2,1)} %copy.121), calls=%async_computation | async-start | bytes 458752 | tf_op jit(solution)/shard_map/all_to_all | solution.py:30
  113.6 0.7 copy.82
  114.4 0.7 copy.83
  115.3 1.0 pad_maximum_fusion.6
  120.8 10.0 %all-to-all-done = bf16[16,1728,4]{1,2,0:T(4,128)(2,1)S(1)} async-done(((bf16[16,1728,4]{1,2,0:T(4,128)(2,1)}), bf16[16,1728,4]{1,2,0:T(4,128)(2,1)S(1)}, u32[]{:S(2)}, u32[]{:S(2)}) %all-to-all-start) | async-done | bytes 221216 | tf_op jit(solution)/shard_map/all_to_all | solution.py:30
  131.1 0.7 copy.122
  131.9 14.9 %all-to-all-start.1 = ((f32[64,27,4]{1,2,0:T(4,128)}), f32[64,27,4]{1,2,0:T(4,128)S(1)}, u32[]{:S(2)}, u32[]{:S(2)}) async-start(f32[64,27,4]{1,2,0:T(4,128)} %copy.122), calls=%async_computation.1 | async-start | bytes 262144 | tf_op jit(solution)/shard_map/all_to_all | solution.py:36
  147.0 0.8 convert_element_type.43
  147.9 0.8 reshape.225
  148.7 12.6 %all-to-all-done.1 = f32[64,27,4]{1,2,0:T(4,128)S(1)} async-done(((f32[64,27,4]{1,2,0:T(4,128)}), f32[64,27,4]{1,2,0:T(4,128)S(1)}, u32[]{:S(2)}, u32[]{:S(2)}) %all-to-all-start.1) | async-done | bytes 27680 | tf_op jit(solution)/shard_map/all_to_all | solution.py:36
  (246 shorter events, 28.5 us)
Async XLA Ops:
  0.6 28.6 %copy-start.9 = (bf16[1,1,16,2048]{3,2,1,0:T(8,128)(2,1)S(1)}, bf16[1,1,16,2048]{3,2,1,0:T(8,128)(2,1)}, u32[]{:S(2)}) copy-start(bf16[1,1,16,2048]{3,2,1,0:T(8,128)(2,1)} %param.3) | copy-start | bytes 196612
  0.6 37.0 %collective-permute-start = (bf16[1,1,16,2048]{3,2,1,0:T(8,128)(2,1)}, bf16[1,1,16,2048]{3,2,1,0:T(8,128)(2,1)S(1)}, u32[]{:S(2)}, u32[]{:S(2)}) collective-permute-start(bf16[1,1,16,2048]{3,2,1,0:T(8,128)(2,1)} %param.3), channel_id=1, source_target_pairs={{0,128},{64,192},{128,256},{192,320},{256,384},{320,448},{384,512}... | collective-permute-start | bytes 196616 | tf_op jit(solution)/shard_map/ppermute | solution.py:56
  6.5 31.1 %collective-permute-start.1 = (bf16[2,1,16,2048]{3,2,1,0:T(8,128)(2,1)S(1)}, bf16[2,1,16,2048]{3,2,1,0:T(8,128)(2,1)S(1)}, u32[]{:S(2)}, u32[]{:S(2)}) collective-permute-start(bf16[2,1,16,2048]{3,2,1,0:T(8,128)(2,1)S(1)} %constant_dynamic-update-slice_fusion), channel_id=1, source_target_pairs={{0,64},{64,128},{128,192},{192,256},{256,320},{320,384},{384,448},... | collective-permute-start | bytes 393224 | tf_op jit(solution)/shard_map/ppermute | solution.py:56
  25.6 22.2 %collective-permute-start.2 = (bf16[2,1,16,2048]{3,2,1,0:T(8,128)(2,1)S(1)}, bf16[2,1,16,2048]{3,2,1,0:T(8,128)(2,1)S(1)}, u32[]{:S(2)}, u32[]{:S(2)}) collective-permute-start(bf16[2,1,16,2048]{3,2,1,0:T(8,128)(2,1)S(1)} %constant_dynamic-update-slice_fusion), channel_id=1, source_target_pairs={{64,0},{128,64},{192,128},{256,192},{320,256},{384,320},{448,384},... | collective-permute-start | bytes 393224 | tf_op jit(solution)/shard_map/ppermute | solution.py:57
  26.9 21.6 %collective-permute-start.3 = (bf16[1,1,16,2048]{3,2,1,0:T(8,128)(2,1)}, bf16[1,1,16,2048]{3,2,1,0:T(8,128)(2,1)S(1)}, u32[]{:S(2)}, u32[]{:S(2)}) collective-permute-start(bf16[1,1,16,2048]{3,2,1,0:T(8,128)(2,1)} %param.3), channel_id=1, source_target_pairs={{128,0},{192,64},{256,128},{320,192},{384,256},{448,320},{512,384}... | collective-permute-start | bytes 196616 | tf_op jit(solution)/shard_map/ppermute | solution.py:57
  37.6 10.9 %copy-start.55 = (bf16[1,1,16,2048]{3,2,1,0:T(8,128)(2,1)}, bf16[1,1,16,2048]{3,2,1,0:T(8,128)(2,1)S(1)}, u32[]{:S(2)}) copy-start(bf16[1,1,16,2048]{3,2,1,0:T(8,128)(2,1)S(1)} %collective-permute-done) | copy-start | bytes 196612
  48.5 5.0 %copy-start.56 = (bf16[1,1,16,2048]{3,2,1,0:T(8,128)(2,1)}, bf16[1,1,16,2048]{3,2,1,0:T(8,128)(2,1)S(1)}, u32[]{:S(2)}) copy-start(bf16[1,1,16,2048]{3,2,1,0:T(8,128)(2,1)S(1)} %collective-permute-done.3) | copy-start | bytes 196612
  69.4 2.0 %copy-start.8 = (bf16[1728,64]{0,1:T(8,128)(2,1)S(1)}, bf16[1728,64]{0,1:T(8,128)(2,1)}, u32[]{:S(2)}) copy-start(bf16[1728,64]{0,1:T(8,128)(2,1)} %param.4) | copy-start | bytes 663556
  69.4 2.4 %copy-start.4 = (bf16[3,16,32,64]{3,2,1,0:T(8,128)(2,1)S(1)}, bf16[3,16,32,64]{3,2,1,0:T(8,128)(2,1)}, u32[]{:S(2)}) copy-start(bf16[3,16,32,64]{3,2,1,0:T(8,128)(2,1)} %get-tuple-element.42) | copy-start | bytes 589828
  82.5 1.6 copy-start.25
  82.5 1.6 copy-start.26
  82.5 1.6 copy-start.27
  85.6 1.9 %copy-start.37 = (bf16[1,16,32,64]{3,2,1,0:T(8,128)(2,1)S(1)}, bf16[1,16,32,64]{3,2,1,0:T(8,128)(2,1)}, u32[]{:S(2)}) copy-start(bf16[1,16,32,64]{3,2,1,0:T(8,128)(2,1)} %get-tuple-element.15) | copy-start | bytes 196612
  85.9 2.4 %copy-start.36 = (bf16[1,16,32,64]{3,2,1,0:T(8,128)(2,1)S(1)}, bf16[1,16,32,64]{3,2,1,0:T(8,128)(2,1)}, u32[]{:S(2)}) copy-start(bf16[1,16,32,64]{3,2,1,0:T(8,128)(2,1)} %get-tuple-element.16) | copy-start | bytes 196612
  85.9 3.1 %copy-start.10 = (bf16[1,16,32,64]{3,2,1,0:T(8,128)(2,1)S(1)}, bf16[1,16,32,64]{3,2,1,0:T(8,128)(2,1)}, u32[]{:S(2)}) copy-start(bf16[1,16,32,64]{3,2,1,0:T(8,128)(2,1)} %get-tuple-element.4) | copy-start | bytes 196612
  85.9 3.1 %copy-start.11 = (bf16[1,16,32,64]{3,2,1,0:T(8,128)(2,1)S(1)}, bf16[1,16,32,64]{3,2,1,0:T(8,128)(2,1)}, u32[]{:S(2)}) copy-start(bf16[1,16,32,64]{3,2,1,0:T(8,128)(2,1)} %get-tuple-element.5) | copy-start | bytes 196612
  85.9 3.1 %copy-start.12 = (bf16[1,16,32,64]{3,2,1,0:T(8,128)(2,1)S(1)}, bf16[1,16,32,64]{3,2,1,0:T(8,128)(2,1)}, u32[]{:S(2)}) copy-start(bf16[1,16,32,64]{3,2,1,0:T(8,128)(2,1)} %get-tuple-element.6) | copy-start | bytes 196612
  85.9 3.1 %copy-start.13 = (bf16[1,16,32,64]{3,2,1,0:T(8,128)(2,1)S(1)}, bf16[1,16,32,64]{3,2,1,0:T(8,128)(2,1)}, u32[]{:S(2)}) copy-start(bf16[1,16,32,64]{3,2,1,0:T(8,128)(2,1)} %get-tuple-element.9) | copy-start | bytes 196612
  85.9 3.1 %copy-start.14 = (bf16[1,16,32,64]{3,2,1,0:T(8,128)(2,1)S(1)}, bf16[1,16,32,64]{3,2,1,0:T(8,128)(2,1)}, u32[]{:S(2)}) copy-start(bf16[1,16,32,64]{3,2,1,0:T(8,128)(2,1)} %get-tuple-element.10) | copy-start | bytes 196612
  85.9 3.1 %copy-start.15 = (bf16[1,16,32,64]{3,2,1,0:T(8,128)(2,1)S(1)}, bf16[1,16,32,64]{3,2,1,0:T(8,128)(2,1)}, u32[]{:S(2)}) copy-start(bf16[1,16,32,64]{3,2,1,0:T(8,128)(2,1)} %get-tuple-element.11) | copy-start | bytes 196612
  88.2 1.7 %copy-start.79 = (bf16[16,4,512]{2,1,0:T(4,128)(2,1)S(1)}, bf16[16,4,512]{2,1,0:T(4,128)(2,1)}, u32[]{:S(2)}) copy-start(bf16[16,4,512]{2,1,0:T(4,128)(2,1)} %dot_general.104) | copy-start | bytes 196612
  89.0 1.8 %copy-start.35 = (bf16[1,16,32,64]{3,2,1,0:T(8,128)(2,1)S(1)}, bf16[1,16,32,64]{3,2,1,0:T(8,128)(2,1)}, u32[]{:S(2)}) copy-start(bf16[1,16,32,64]{3,2,1,0:T(8,128)(2,1)} %get-tuple-element.8) | copy-start | bytes 196612
  89.0 2.5 %copy-start.34 = (bf16[1,16,32,64]{3,2,1,0:T(8,128)(2,1)S(1)}, bf16[1,16,32,64]{3,2,1,0:T(8,128)(2,1)}, u32[]{:S(2)}) copy-start(bf16[1,16,32,64]{3,2,1,0:T(8,128)(2,1)} %get-tuple-element.7) | copy-start | bytes 196612
  89.9 2.3 %copy-start.43 = (bf16[512,64]{1,0:T(8,128)(2,1)S(1)}, bf16[512,64]{1,0:T(8,128)(2,1)}, u32[]{:S(2)}) copy-start(bf16[512,64]{1,0:T(8,128)(2,1)} %concatenate.201) | copy-start | bytes 196612
  89.9 3.0 %copy-start.54 = (bf16[1,16,32,192]{3,2,1,0:T(8,128)(2,1)S(1)}, bf16[1,16,32,192]{3,2,1,0:T(8,128)(2,1)}, u32[]{:S(2)}) copy-start(bf16[1,16,32,192]{3,2,1,0:T(8,128)(2,1)} %get-tuple-element.106) | copy-start | bytes 589828
  89.9 3.0 %copy-start.80 = (bf16[16,4,512]{2,1,0:T(4,128)(2,1)S(1)}, bf16[16,4,512]{2,1,0:T(4,128)(2,1)}, u32[]{:S(2)}) copy-start(bf16[16,4,512]{2,1,0:T(4,128)(2,1)} %dot_general.104) | copy-start | bytes 196612
  90.0 3.8 %copy-start.33 = (bf16[1,16,32,64]{3,2,1,0:T(8,128)(2,1)S(1)}, bf16[1,16,32,64]{3,2,1,0:T(8,128)(2,1)}, u32[]{:S(2)}) copy-start(bf16[1,16,32,64]{3,2,1,0:T(8,128)(2,1)} %get-tuple-element.24) | copy-start | bytes 196612
  90.0 3.9 %copy-start.32 = (bf16[1,16,32,64]{3,2,1,0:T(8,128)(2,1)S(1)}, bf16[1,16,32,64]{3,2,1,0:T(8,128)(2,1)}, u32[]{:S(2)}) copy-start(bf16[1,16,32,64]{3,2,1,0:T(8,128)(2,1)} %get-tuple-element.25) | copy-start | bytes 196612
  90.8 3.2 %copy-start.42 = (bf16[512,64]{1,0:T(8,128)(2,1)S(1)}, bf16[512,64]{1,0:T(8,128)(2,1)}, u32[]{:S(2)}) copy-start(bf16[512,64]{1,0:T(8,128)(2,1)} %concatenate.213) | copy-start | bytes 196612
  91.5 2.6 %copy-start.63 = (bf16[512,64]{0,1:T(8,128)(2,1)S(1)}, bf16[512,64]{0,1:T(8,128)(2,1)}, u32[]{:S(2)}) copy-start(bf16[512,64]{0,1:T(8,128)(2,1)} %copy.108) | copy-start | bytes 196612
  91.5 2.6 %copy-start.70 = (bf16[512,64]{0,1:T(8,128)(2,1)S(1)}, bf16[512,64]{0,1:T(8,128)(2,1)}, u32[]{:S(2)}) copy-start(bf16[512,64]{0,1:T(8,128)(2,1)} %copy.107) | copy-start | bytes 196612
  91.5 2.6 %copy-start.71 = (bf16[512,64]{0,1:T(8,128)(2,1)S(1)}, bf16[512,64]{0,1:T(8,128)(2,1)}, u32[]{:S(2)}) copy-start(bf16[512,64]{0,1:T(8,128)(2,1)} %copy.109) | copy-start | bytes 196612
  92.9 2.3 %copy-start.75 = (bf16[512,64]{0,1:T(8,128)(2,1)S(1)}, bf16[512,64]{0,1:T(8,128)(2,1)}, u32[]{:S(2)}) copy-start(bf16[512,64]{0,1:T(8,128)(2,1)} %copy.101) | copy-start | bytes 196612
  92.9 2.3 %copy-start.76 = (bf16[512,64]{0,1:T(8,128)(2,1)S(1)}, bf16[512,64]{0,1:T(8,128)(2,1)}, u32[]{:S(2)}) copy-start(bf16[512,64]{0,1:T(8,128)(2,1)} %copy.99) | copy-start | bytes 196612
  93.9 2.4 %copy-start.81 = (bf16[16,4,512]{2,1,0:T(4,128)(2,1)S(1)}, bf16[16,4,512]{2,1,0:T(4,128)(2,1)}, u32[]{:S(2)}) copy-start(bf16[16,4,512]{2,1,0:T(4,128)(2,1)} %dot_general.104) | copy-start | bytes 196612
  94.1 2.4 %copy-start.67 = (f32[192,16,4]{0,1,2:T(8,128)S(1)}, f32[192,16,4]{0,1,2:T(8,128)}, u32[]{:S(2)}) copy-start(f32[192,16,4]{0,1,2:T(8,128)} %fusion.53) | copy-start | bytes 147460
  94.1 2.4 %copy-start.68 = (f32[192,16,4]{0,1,2:T(8,128)S(1)}, f32[192,16,4]{0,1,2:T(8,128)}, u32[]{:S(2)}) copy-start(f32[192,16,4]{0,1,2:T(8,128)} %fusion.56) | copy-start | bytes 147460
  94.1 2.4 %copy-start.69 = (f32[192,16,4]{0,1,2:T(8,128)S(1)}, f32[192,16,4]{0,1,2:T(8,128)}, u32[]{:S(2)}) copy-start(f32[192,16,4]{0,1,2:T(8,128)} %fusion.58) | copy-start | bytes 147460
  94.2 2.4 %copy-start.74 = (f32[192,16,4]{0,1,2:T(8,128)S(1)}, f32[192,16,4]{0,1,2:T(8,128)}, u32[]{:S(2)}) copy-start(f32[192,16,4]{0,1,2:T(8,128)} %fusion.61) | copy-start | bytes 147460
  96.7 17.7 %copy-start.40 = (bf16[1,16,32,64]{3,2,1,0:T(8,128)(2,1)S(1)}, bf16[1,16,32,64]{3,2,1,0:T(8,128)(2,1)}, u32[]{:S(2)}) copy-start(bf16[1,16,32,64]{3,2,1,0:T(8,128)(2,1)} %get-tuple-element.55) | copy-start | bytes 196612
  96.8 16.9 %copy-start.41 = (bf16[1,16,32,64]{3,2,1,0:T(8,128)(2,1)S(1)}, bf16[1,16,32,64]{3,2,1,0:T(8,128)(2,1)}, u32[]{:S(2)}) copy-start(bf16[1,16,32,64]{3,2,1,0:T(8,128)(2,1)} %get-tuple-element.54) | copy-start | bytes 196612
  96.8 18.3 %copy-start.39 = (bf16[1,16,32,64]{3,2,1,0:T(8,128)(2,1)S(1)}, bf16[1,16,32,64]{3,2,1,0:T(8,128)(2,1)}, u32[]{:S(2)}) copy-start(bf16[1,16,32,64]{3,2,1,0:T(8,128)(2,1)} %get-tuple-element.62) | copy-start | bytes 196612
  96.8 18.4 %copy-start.38 = (bf16[1,16,32,64]{3,2,1,0:T(8,128)(2,1)S(1)}, bf16[1,16,32,64]{3,2,1,0:T(8,128)(2,1)}, u32[]{:S(2)}) copy-start(bf16[1,16,32,64]{3,2,1,0:T(8,128)(2,1)} %get-tuple-element.63) | copy-start | bytes 196612
  96.8 18.5 %copy-start.30 = (bf16[1,16,32,64]{3,2,1,0:T(8,128)(2,1)S(1)}, bf16[1,16,32,64]{3,2,1,0:T(8,128)(2,1)}, u32[]{:S(2)}) copy-start(bf16[1,16,32,64]{3,2,1,0:T(8,128)(2,1)} %get-tuple-element.52) | copy-start | bytes 196612
  96.8 18.5 %copy-start.31 = (bf16[1,16,32,64]{3,2,1,0:T(8,128)(2,1)S(1)}, bf16[1,16,32,64]{3,2,1,0:T(8,128)(2,1)}, u32[]{:S(2)}) copy-start(bf16[1,16,32,64]{3,2,1,0:T(8,128)(2,1)} %get-tuple-element.53) | copy-start | bytes 196612
  97.6 33.3 %all-to-all-start = ((bf16[16,1728,4]{1,2,0:T(4,128)(2,1)}), bf16[16,1728,4]{1,2,0:T(4,128)(2,1)S(1)}, u32[]{:S(2)}, u32[]{:S(2)}) async-start(bf16[16,1728,4]{1,2,0:T(4,128)(2,1)} %copy.121), calls=%async_computation | async-start | bytes 458752 | tf_op jit(solution)/shard_map/all_to_all | solution.py:30
  113.6 2.8 %copy-start.61 = (bf16[3,64,64]{2,1,0:T(8,128)(2,1)S(1)}, bf16[3,64,64]{2,1,0:T(8,128)(2,1)}, u32[]{:S(2)}) copy-start(bf16[3,64,64]{2,1,0:T(8,128)(2,1)} %copy.81) | copy-start | bytes 73732
  131.9 29.5 %all-to-all-start.1 = ((f32[64,27,4]{1,2,0:T(4,128)}), f32[64,27,4]{1,2,0:T(4,128)S(1)}, u32[]{:S(2)}, u32[]{:S(2)}) async-start(f32[64,27,4]{1,2,0:T(4,128)} %copy.122), calls=%async_computation.1 | async-start | bytes 262144 | tf_op jit(solution)/shard_map/all_to_all | solution.py:36
  (43 other events, 46.2 us)

commit v2 on v0

--- a/solution.py
+++ b/solution.py
@@ -52,56 +52,37 @@
     height = volume.shape[2]
     width = volume.shape[3] // chans
     cells = planes * height * width
+    kern = weight.reshape(3, 3, 3, chans, chans)
+    dims = ("NDHWC", "DHWIO", "NDHWC")
+    same = [(0, 0), (1, 1), (1, 1)]
     extended = padded_2(volume, (("dp", 1),), 1)
-    padded = jnp.pad(
-        extended.reshape(planes + 2, height, width, chans), ((0, 0), (1, 1), (1, 1), (0, 0))
-    )
-    blocks = []
-    flipped = []
-    for tap_z in range(3):
-        for tap_y in range(3):
-            first = (tap_z * 3 + tap_y) * 3 * chans
-            block = weight[first : first + 3 * chans]
-            blocks.append(block)
-            flipped.append(
-                block.reshape(3, chans, chans).transpose(0, 2, 1).reshape(3 * chans, chans)
-            )
-    pre = jnp.zeros((cells, chans), jnp.float32)
-    for tap_z in range(3):
-        for tap_y in range(3):
-            window = strips(padded, tap_z, tap_y, planes, height, width, (0, 1, 2))
-            pre = pre + jnp.dot(
-                window, blocks[tap_z * 3 + tap_y], preferred_element_type=jnp.float32
-            )
+    v_ext = extended.reshape(1, planes + 2, height, width, chans)
+    pre = lax.conv_general_dilated(
+        v_ext, kern, (1, 1, 1), same, dimension_numbers=dims, preferred_element_type=jnp.float32
+    ).reshape(cells, chans)
     sig = jax.nn.sigmoid(pre)
     activation = (pre * sig).astype(jnp.bfloat16).reshape(1, planes, height, width * chans)
     delta = (
         cotangent.reshape(cells, chans).astype(jnp.float32) * sig * (1.0 + pre * (1.0 - sig))
     ).astype(jnp.bfloat16)
     delta_ext = padded_2(delta.reshape(1, planes, height, width * chans), (("dp", 1),), 1)
-    delta_pad = jnp.pad(
-        delta_ext.reshape(planes + 2, height, width, chans), ((0, 0), (1, 1), (1, 1), (0, 0))
+    d_ext = delta_ext.reshape(1, planes + 2, height, width, chans)
+    flipped = jnp.flip(kern, (0, 1, 2)).transpose(0, 1, 2, 4, 3)
+    back = lax.conv_general_dilated(
+        d_ext, flipped, (1, 1, 1), same, dimension_numbers=dims, preferred_element_type=jnp.float32
     )
-    back = jnp.zeros((cells, chans), jnp.float32)
-    for tap_z in range(3):
-        for tap_y in range(3):
-            window = strips(delta_pad, 2 - tap_z, 2 - tap_y, planes, height, width, (2, 1, 0))
-            back = back + jnp.dot(
-                window, flipped[tap_z * 3 + tap_y], preferred_element_type=jnp.float32
-            )
-    summed = back.reshape(planes, height, width * chans)
-    input_grad = summed.astype(jnp.bfloat16).reshape(1, planes, height, width * chans)
-    pieces = []
-    for tap_z in range(3):
-        for tap_y in range(3):
-            window = strips(padded, tap_z, tap_y, planes, height, width, (0, 1, 2))
-            pieces.append(
-                lax.dot_general(
-                    window, delta, (((0,), (0,)), ((), ())), preferred_element_type=jnp.float32
-                )
-            )
+    input_grad = back.astype(jnp.bfloat16).reshape(1, planes, height, width * chans)
+    v_pad = jnp.pad(v_ext, ((0, 0), (0, 0), (1, 1), (1, 1), (0, 0)))
+    grads = lax.conv_general_dilated(
+        v_pad,
+        delta.reshape(1, planes, height, width, chans),
+        (1, 1, 1),
+        [(0, 0), (0, 0), (0, 0)],
+        dimension_numbers=("CDHWN", "IDHWO", "NDHWC"),
+        preferred_element_type=jnp.float32,
+    )
     scale = 1.0 / math.sqrt(lax.axis_size("dp") * lax.axis_size("gz") * cells)
-    terms = jnp.concatenate(pieces, axis=0) * scale
+    terms = grads.transpose(1, 2, 3, 0, 4).reshape(27 * chans, chans) * scale
     reduced = sum_at_owner(terms.astype(jnp.bfloat16), "dp", 1)
     weight_grad = sum_at_owner_2(reduced, "gz", 0)
     return (activation, input_grad, weight_grad)

time: 131 us -> 119 us (0.908)
  the two profiles are of different devices: /device:TPU:1 before, /device:TPU:32 now
where the time goes in v2:
time: 119 us; the launch traced here: 118 us
  starting transfers between devices  59.4 us (50%)
  waiting for transfers between devices  40.2 us (34%)
  local copies, waits for them, and re-layouts  9.88 us (8%)
  matrix products  5.84 us (5%)
  other arithmetic  1.75 us (1%)
    ppermute x2, starting transfers between devices, padded_2(): lax.ppermute(lax.slice_in_dim(block, block.shape[dim] - width, None, axis...  22 us
    ppermute x2, waiting for transfers between devices, padded_2(): lax.ppermute(lax.slice_in_dim(block, 0, width, axis=dim), axis, backward)  17.5 us
    all_to_all x1, starting transfers between devices, sum_at_owner_2(): lax.all_to_all(pieces, axis, split_axis=0, concat_axis=0, tiled=True)  15.9 us
    ppermute x2, starting transfers between devices, padded_2(): lax.ppermute(lax.slice_in_dim(block, 0, width, axis=dim), axis, backward)  14 us
    all_to_all x1, waiting for transfers between devices, sum_at_owner_2(): lax.all_to_all(pieces, axis, split_axis=0, concat_axis=0, tiled=True)  12.6 us
    ppermute x2, waiting for transfers between devices, padded_2(): lax.ppermute(lax.slice_in_dim(block, block.shape[dim] - width, None, axis...  10 us
    all_to_all x1, starting transfers between devices, sum_at_owner(): pieces = lax.all_to_all(split_up(value, dim, size), axis, 0, 0, tiled=True)  7.54 us
    transpose x1, matrix products, per_device(): terms = grads.transpose(1, 2, 3, 0, 4).reshape(27 * chans, chans) * scale  3.73 us
  transfers between devices with their start and end apart: 6, of which 5 were waited for; matrix products, arithmetic and copies ran while one was open for 5% of the time, Pallas kernels for 0%

profile of v2, /device:TPU:32, one launch (start us, length us, event | category | flops | bytes accessed | tf_op | source)
XLA Modules:
  0.0 118.0 jit_solution(1563986936398307091)
XLA Ops:
  0.6 19.5 %collective-permute-start = (bf16[1,1,16,2048]{3,2,1,0:T(8,128)(2,1)}, bf16[1,1,16,2048]{3,2,1,0:T(8,128)(2,1)S(1)}, u32[]{:S(2)}, u32[]{:S(2)}) collective-permute-start(bf16[1,1,16,2048]{3,2,1,0:T(8,128)(2,1)} %param.3), channel_id=1, source_target_pairs={{0,64},{64,128},{128,192},{192,256},{256,320},{320,384},{384,448},... | collective-permute-start | bytes 196616 | tf_op jit(solution)/shard_map/ppermute | solution.py:14
  20.1 1.9 %collective-permute-start.1 = (bf16[1,1,16,2048]{3,2,1,0:T(8,128)(2,1)}, bf16[1,1,16,2048]{3,2,1,0:T(8,128)(2,1)S(1)}, u32[]{:S(2)}, u32[]{:S(2)}) collective-permute-start(bf16[1,1,16,2048]{3,2,1,0:T(8,128)(2,1)} %param.3), channel_id=1, source_target_pairs={{64,0},{128,64},{192,128},{256,192},{320,256},{384,320},{448,384},... | collective-permute-start | bytes 196616 | tf_op jit(solution)/shard_map/ppermute | solution.py:17
  22.1 1.2 %copy.61 = bf16[1728,64]{1,0:T(8,128)(2,1)S(1)} copy(bf16[1728,64]{0,1:T(8,128)(2,1)} %param.4) | data formatting | bytes 442368 | tf_op jit(solution)/shard_map/reshape | solution.py:55
  23.3 1.0 reshape.123
  24.3 0.9 collective-permute-done
  25.2 11.7 %collective-permute-done.1 = bf16[1,1,16,2048]{3,2,1,0:T(8,128)(2,1)S(1)} collective-permute-done((bf16[1,1,16,2048]{3,2,1,0:T(8,128)(2,1)}, bf16[1,1,16,2048]{3,2,1,0:T(8,128)(2,1)S(1)}, u32[]{:S(2)}, u32[]{:S(2)}) %collective-permute-start.1) | collective-permute-done | bytes 65568 | tf_op jit(solution)/shard_map/ppermute | solution.py:17
  36.9 0.4 reshape.124
  37.3 0.6 reshape.141
  37.9 0.2 copy.64
  38.1 0.1 pad.2.clone
  38.2 0.0 copy-start.2
  38.2 0.1 copy.43
  38.3 0.1 slice.6
  38.4 0.5 copy-done.2
  38.8 0.8 add_divide_fusion
  39.7 0.1 copy.55
  39.8 0.1 copy.53
  39.9 0.2 fusion.19
  40.1 3.7 %fusion.2 = bf16[3,3,3,64,64]{4,3,2,1,0:T(8,128)(2,1)S(1)} fusion(bf16[1,3,16,32,64]{4,0,3,2,1:T(2,128)(2,1)S(1)} %reshape.141, bf16[1,1,16,32,64]{4,3,2,1,0:T(8,128)(2,1)S(1)} %fusion.19), kind=kOutput, calls=%fused_computation.4 | convolution fusion | flops 106487808 | bytes 483328 | tf_op jit(solution)/shard_map/transpose | solution.py:85
  43.8 1.0 copy.59
  44.8 1.1 convert_element_type.56
  45.8 7.5 %all-to-all-start = ((bf16[16,1728,4]{1,2,0:T(4,128)(2,1)}), bf16[16,1728,4]{1,2,0:T(4,128)(2,1)S(1)}, u32[]{:S(2)}, u32[]{:S(2)}) async-start(bf16[16,1728,4]{1,2,0:T(4,128)(2,1)} %bitcast.12), calls=%async_computation | async-start | bytes 458752 | tf_op jit(solution)/shard_map/all_to_all | solution.py:30
  53.4 0.1 copy.45
  53.4 0.0 copy-start
  53.5 0.1 copy.46
  53.6 0.1 reshape.102
  53.7 0.6 copy-done
  54.3 0.7 multiply_convert_fusion
  55.0 12.1 %collective-permute-start.3 = (bf16[1,1,16,2048]{3,2,1,0:T(8,128)(2,1)S(1)}, bf16[1,1,16,2048]{3,2,1,0:T(8,128)(2,1)S(1)}, u32[]{:S(2)}, u32[]{:S(2)}) collective-permute-start(bf16[1,1,16,2048]{3,2,1,0:T(8,128)(2,1)S(1)} %get-tuple-element.5), channel_id=1, source_target_pairs={{64,0},{128,64},{192,128},{256,192},{320,256},{384,320},{448,384},... | collective-permute-start | bytes 196616 | tf_op jit(solution)/shard_map/ppermute | solution.py:17
  67.1 2.5 %collective-permute-start.2 = (bf16[1,1,16,2048]{3,2,1,0:T(8,128)(2,1)S(1)}, bf16[1,1,16,2048]{3,2,1,0:T(8,128)(2,1)S(1)}, u32[]{:S(2)}, u32[]{:S(2)}) collective-permute-start(bf16[1,1,16,2048]{3,2,1,0:T(8,128)(2,1)S(1)} %get-tuple-element.5), channel_id=1, source_target_pairs={{0,64},{64,128},{128,192},{192,256},{256,320},{320,384},{384,448},... | collective-permute-start | bytes 196616 | tf_op jit(solution)/shard_map/ppermute | solution.py:14
  69.5 0.2 concatenate.15
  69.7 5.8 %collective-permute-done.3 = bf16[1,1,16,2048]{3,2,1,0:T(8,128)(2,1)S(1)} collective-permute-done((bf16[1,1,16,2048]{3,2,1,0:T(8,128)(2,1)S(1)}, bf16[1,1,16,2048]{3,2,1,0:T(8,128)(2,1)S(1)}, u32[]{:S(2)}, u32[]{:S(2)}) %collective-permute-start.3) | collective-permute-done | bytes 65568 | tf_op jit(solution)/shard_map/ppermute | solution.py:17
  75.5 0.2 concatenate.16
  75.7 9.1 %collective-permute-done.2 = bf16[1,1,16,2048]{3,2,1,0:T(8,128)(2,1)S(1)} collective-permute-done((bf16[1,1,16,2048]{3,2,1,0:T(8,128)(2,1)S(1)}, bf16[1,1,16,2048]{3,2,1,0:T(8,128)(2,1)S(1)}, u32[]{:S(2)}, u32[]{:S(2)}) %collective-permute-start.2) | collective-permute-done | bytes 65568 | tf_op jit(solution)/shard_map/ppermute | solution.py:14
  84.9 0.2 concatenate.14
  85.0 0.1 maximum_bitcast_fusion
  85.1 0.2 copy.65
  85.3 0.1 pad.4.clone
  85.4 0.1 copy.49
  85.5 0.1 slice.8
  85.6 0.1 convert_reduce_fusion
  85.7 0.2 reshape.104
  85.9 0.7 copy.60
  86.6 15.9 %all-to-all-start.1 = ((f32[64,27,4]{1,2,0:T(4,128)}), f32[64,27,4]{1,2,0:T(4,128)S(1)}, u32[]{:S(2)}, u32[]{:S(2)}) async-start(f32[64,27,4]{1,2,0:T(4,128)} %copy.60), calls=%async_computation.1 | async-start | bytes 262144 | tf_op jit(solution)/shard_map/all_to_all | solution.py:36
  102.6 1.3 %fusion.3 = bf16[1,16,8,5,64]{4,2,3,1,0:T(8,128)(2,1)S(1)} fusion(bf16[3,3,3,64,64]{4,3,2,1,0:T(8,128)(2,1)S(1)} %bitcast.64, bf16[3,16,1,7,2,64]{5,3,4,1,0,2:T(8,128)(2,1)S(1)} %slice.8, bf16[3,16,1,8,5,64]{5,3,4,1,0,2:T(8,128)(2,1)S(1)} %copy.49, pred[8,5]{0,1:T(8,128)(4,1)S(1)} %copy-done.2), kind=kOutput, calls=%fused_computation.7 | convolution fusion | flops 136773632 | bytes 634920 | tf_op jit(solution)/shard_map/conv_general_dilated | solution.py:71
  104.0 0.8 reshape.103
  104.8 12.6 %all-to-all-done.1 = f32[64,27,4]{1,2,0:T(4,128)S(1)} async-done(((f32[64,27,4]{1,2,0:T(4,128)}), f32[64,27,4]{1,2,0:T(4,128)S(1)}, u32[]{:S(2)}, u32[]{:S(2)}) %all-to-all-start.1) | async-done | bytes 27680 | tf_op jit(solution)/shard_map/all_to_all | solution.py:36
  117.4 0.7 reduce_sum.19
  (12 shorter events, 0.2 us)
Async XLA Ops:
  0.6 24.6 %copy-start.1 = (bf16[1,1,16,2048]{3,2,1,0:T(8,128)(2,1)S(1)}, bf16[1,1,16,2048]{3,2,1,0:T(8,128)(2,1)}, u32[]{:S(2)}) copy-start(bf16[1,1,16,2048]{3,2,1,0:T(8,128)(2,1)} %param.3) | copy-start | bytes 196612
  0.6 24.6 %collective-permute-start = (bf16[1,1,16,2048]{3,2,1,0:T(8,128)(2,1)}, bf16[1,1,16,2048]{3,2,1,0:T(8,128)(2,1)S(1)}, u32[]{:S(2)}, u32[]{:S(2)}) collective-permute-start(bf16[1,1,16,2048]{3,2,1,0:T(8,128)(2,1)} %param.3), channel_id=1, source_target_pairs={{0,64},{64,128},{128,192},{192,256},{256,320},{320,384},{384,448},... | collective-permute-start | bytes 196616 | tf_op jit(solution)/shard_map/ppermute | solution.py:14
  20.1 16.8 %collective-permute-start.1 = (bf16[1,1,16,2048]{3,2,1,0:T(8,128)(2,1)}, bf16[1,1,16,2048]{3,2,1,0:T(8,128)(2,1)S(1)}, u32[]{:S(2)}, u32[]{:S(2)}) collective-permute-start(bf16[1,1,16,2048]{3,2,1,0:T(8,128)(2,1)} %param.3), channel_id=1, source_target_pairs={{64,0},{128,64},{192,128},{256,192},{320,256},{384,320},{448,384},... | collective-permute-start | bytes 196616 | tf_op jit(solution)/shard_map/ppermute | solution.py:17
  38.2 0.7 copy-start.2
  45.8 39.8 %all-to-all-start = ((bf16[16,1728,4]{1,2,0:T(4,128)(2,1)}), bf16[16,1728,4]{1,2,0:T(4,128)(2,1)S(1)}, u32[]{:S(2)}, u32[]{:S(2)}) async-start(bf16[16,1728,4]{1,2,0:T(4,128)(2,1)} %bitcast.12), calls=%async_computation | async-start | bytes 458752 | tf_op jit(solution)/shard_map/all_to_all | solution.py:30
  53.4 0.8 copy-start
  55.0 20.6 %collective-permute-start.3 = (bf16[1,1,16,2048]{3,2,1,0:T(8,128)(2,1)S(1)}, bf16[1,1,16,2048]{3,2,1,0:T(8,128)(2,1)S(1)}, u32[]{:S(2)}, u32[]{:S(2)}) collective-permute-start(bf16[1,1,16,2048]{3,2,1,0:T(8,128)(2,1)S(1)} %get-tuple-element.5), channel_id=1, source_target_pairs={{64,0},{128,64},{192,128},{256,192},{320,256},{384,320},{448,384},... | collective-permute-start | bytes 196616 | tf_op jit(solution)/shard_map/ppermute | solution.py:17
  67.1 17.8 %collective-permute-start.2 = (bf16[1,1,16,2048]{3,2,1,0:T(8,128)(2,1)S(1)}, bf16[1,1,16,2048]{3,2,1,0:T(8,128)(2,1)S(1)}, u32[]{:S(2)}, u32[]{:S(2)}) collective-permute-start(bf16[1,1,16,2048]{3,2,1,0:T(8,128)(2,1)S(1)} %get-tuple-element.5), channel_id=1, source_target_pairs={{0,64},{64,128},{128,192},{192,256},{256,320},{320,384},{384,448},... | collective-permute-start | bytes 196616 | tf_op jit(solution)/shard_map/ppermute | solution.py:14
  86.6 30.7 %all-to-all-start.1 = ((f32[64,27,4]{1,2,0:T(4,128)}), f32[64,27,4]{1,2,0:T(4,128)S(1)}, u32[]{:S(2)}, u32[]{:S(2)}) async-start(f32[64,27,4]{1,2,0:T(4,128)} %copy.60), calls=%async_computation.1 | async-start | bytes 262144 | tf_op jit(solution)/shard_map/all_to_all | solution.py:36

commit v3 on v2

--- a/solution.py
+++ b/solution.py
@@ -46,33 +46,58 @@
     return joined.reshape(planes * height * width, joined.shape[-1])
 
 
+def halo_planes(block, axis, depth):
+    count = lax.axis_size(axis)
+    planes = block.shape[1]
+    below, above = [], []
+    for shift in range(1, -(-depth // planes) + 1):
+        forward = [(i, i + shift) for i in range(count - shift)]
+        backward = [(target, source) for source, target in forward]
+        below.insert(0, lax.ppermute(block, axis, forward))
+        above.append(lax.ppermute(block, axis, backward))
+    low = jnp.concatenate(below, axis=1)
+    high = jnp.concatenate(above, axis=1)
+    low = lax.slice_in_dim(low, low.shape[1] - depth, None, axis=1)
+    high = lax.slice_in_dim(high, 0, depth, axis=1)
+    return low, high
+
+
 def per_device(volume, weight, cotangent):
     chans = weight.shape[1]
     planes = volume.shape[1]
     height = volume.shape[2]
     width = volume.shape[3] // chans
     cells = planes * height * width
+    ext = planes + 2
     kern = weight.reshape(3, 3, 3, chans, chans)
     dims = ("NDHWC", "DHWIO", "NDHWC")
     same = [(0, 0), (1, 1), (1, 1)]
-    extended = padded_2(volume, (("dp", 1),), 1)
-    v_ext = extended.reshape(1, planes + 2, height, width, chans)
+    both = jnp.concatenate([volume, cotangent], axis=0)
+    low1, high1 = halo_planes(both, "dp", 1)
+    low2, high2 = halo_planes(volume, "dp", 2)
+    v_ext = jnp.concatenate([low2[:, :1], low1[:1], volume, high1[:1], high2[:, 1:]], axis=1)
+    c_ext = jnp.concatenate([low1[1:], cotangent, high1[1:]], axis=1)
+    v_ext = v_ext.reshape(1, planes + 4, height, width, chans)
     pre = lax.conv_general_dilated(
         v_ext, kern, (1, 1, 1), same, dimension_numbers=dims, preferred_element_type=jnp.float32
-    ).reshape(cells, chans)
+    ).reshape(ext * height * width, chans)
     sig = jax.nn.sigmoid(pre)
-    activation = (pre * sig).astype(jnp.bfloat16).reshape(1, planes, height, width * chans)
-    delta = (
-        cotangent.reshape(cells, chans).astype(jnp.float32) * sig * (1.0 + pre * (1.0 - sig))
+    inner = slice(height * width, (planes + 1) * height * width)
+    activation = (pre[inner] * sig[inner]).astype(jnp.bfloat16)
+    activation = activation.reshape(1, planes, height, width * chans)
+    delta_ext = (
+        c_ext.reshape(ext * height * width, chans).astype(jnp.float32)
+        * sig
+        * (1.0 + pre * (1.0 - sig))
     ).astype(jnp.bfloat16)
-    delta_ext = padded_2(delta.reshape(1, planes, height, width * chans), (("dp", 1),), 1)
-    d_ext = delta_ext.reshape(1, planes + 2, height, width, chans)
+    delta = delta_ext[inner]
+    d_ext = delta_ext.reshape(1, ext, height, width, chans)
     flipped = jnp.flip(kern, (0, 1, 2)).transpose(0, 1, 2, 4, 3)
     back = lax.conv_general_dilated(
         d_ext, flipped, (1, 1, 1), same, dimension_numbers=dims, preferred_element_type=jnp.float32
     )
     input_grad = back.astype(jnp.bfloat16).reshape(1, planes, height, width * chans)
-    v_pad = jnp.pad(v_ext, ((0, 0), (0, 0), (1, 1), (1, 1), (0, 0)))
+    v_pad = jnp.pad(v_ext[:, 1 : 1 + ext], ((0, 0), (0, 0), (1, 1), (1, 1), (0, 0)))
     grads = lax.conv_general_dilated(
         v_pad,
         delta.reshape(1, planes, height, width, chans),

time: 119 us -> 130 us (1.092)
  the two profiles are of different devices: /device:TPU:32 before, /device:TPU:1 now
where the time goes in v3:
time: 130 us; the launch traced here: 129 us
  starting transfers between devices  56.7 us (44%)
  waiting for transfers between devices  44.4 us (34%)
  local copies, waits for them, and re-layouts  16.8 us (13%)
  matrix products  8.42 us (6%)
  other arithmetic  1.59 us (1%)
    ppermute x2, starting transfers between devices, halo_planes(): below.insert(0, lax.ppermute(block, axis, forward))  23.2 us
    ppermute x2, waiting for transfers between devices, halo_planes(): above.append(lax.ppermute(block, axis, backward))  18.3 us
    all_to_all x1, starting transfers between devices, sum_at_owner(): pieces = lax.all_to_all(split_up(value, dim, size), axis, 0, 0, tiled=True)  16 us
    all_to_all x1, starting transfers between devices, sum_at_owner_2(): lax.all_to_all(pieces, axis, split_axis=0, concat_axis=0, tiled=True)  14.9 us
    all_to_all x1, waiting for transfers between devices, sum_at_owner(): pieces = lax.all_to_all(split_up(value, dim, size), axis, 0, 0, tiled=True)  14.5 us
    all_to_all x1, waiting for transfers between devices, sum_at_owner_2(): lax.all_to_all(pieces, axis, split_axis=0, concat_axis=0, tiled=True)  11.5 us
    unnamed x21, local copies, waits for them, and re-layouts  4.26 us
    transpose x1, matrix products, per_device(): terms = grads.transpose(1, 2, 3, 0, 4).reshape(27 * chans, chans) * scale  3.85 us
  transfers between devices with their start and end apart: 6, of which 3 were waited for; matrix products, arithmetic and copies ran while one was open for 6% of the time, Pallas kernels for 0%

profile of v3, /device:TPU:1, one launch (start us, length us, event | category | flops | bytes accessed | tf_op | source)
XLA Modules:
  0.0 129.0 jit_solution(16216241776838764077)
XLA Ops:
  0.6 4.2 %collective-permute-start = (bf16[1,1,16,2048]{3,2,1,0:T(8,128)(2,1)}, bf16[1,1,16,2048]{3,2,1,0:T(8,128)(2,1)S(1)}, u32[]{:S(2)}, u32[]{:S(2)}) collective-permute-start(bf16[1,1,16,2048]{3,2,1,0:T(8,128)(2,1)} %param.3), channel_id=1, source_target_pairs={{0,128},{64,192},{128,256},{192,320},{256,384},{320,448},{384,512}... | collective-permute-start | bytes 196616 | tf_op jit(solution)/shard_map/ppermute | solution.py:56
  4.8 0.9 constant_dynamic-update-slice_fusion.1
  5.7 0.8 constant_dynamic-update-slice_fusion
  6.5 19.1 %collective-permute-start.1 = (bf16[2,1,16,2048]{3,2,1,0:T(8,128)(2,1)S(1)}, bf16[2,1,16,2048]{3,2,1,0:T(8,128)(2,1)S(1)}, u32[]{:S(2)}, u32[]{:S(2)}) collective-permute-start(bf16[2,1,16,2048]{3,2,1,0:T(8,128)(2,1)S(1)} %constant_dynamic-update-slice_fusion), channel_id=1, source_target_pairs={{0,64},{64,128},{128,192},{192,256},{256,320},{320,384},{384,448},... | collective-permute-start | bytes 393224 | tf_op jit(solution)/shard_map/ppermute | solution.py:56
  25.6 1.3 %collective-permute-start.2 = (bf16[2,1,16,2048]{3,2,1,0:T(8,128)(2,1)S(1)}, bf16[2,1,16,2048]{3,2,1,0:T(8,128)(2,1)S(1)}, u32[]{:S(2)}, u32[]{:S(2)}) collective-permute-start(bf16[2,1,16,2048]{3,2,1,0:T(8,128)(2,1)S(1)} %constant_dynamic-update-slice_fusion), channel_id=1, source_target_pairs={{64,0},{128,64},{192,128},{256,192},{320,256},{384,320},{448,384},... | collective-permute-start | bytes 393224 | tf_op jit(solution)/shard_map/ppermute | solution.py:57
  26.9 1.3 %collective-permute-start.3 = (bf16[1,1,16,2048]{3,2,1,0:T(8,128)(2,1)}, bf16[1,1,16,2048]{3,2,1,0:T(8,128)(2,1)S(1)}, u32[]{:S(2)}, u32[]{:S(2)}) collective-permute-start(bf16[1,1,16,2048]{3,2,1,0:T(8,128)(2,1)} %param.3), channel_id=1, source_target_pairs={{128,0},{192,64},{256,128},{320,192},{384,256},{448,320},{512,384}... | collective-permute-start | bytes 196616 | tf_op jit(solution)/shard_map/ppermute | solution.py:57
  28.2 1.2 copy.65
  29.5 18.3 %collective-permute-done.2 = bf16[2,1,16,2048]{3,2,1,0:T(8,128)(2,1)S(1)} collective-permute-done((bf16[2,1,16,2048]{3,2,1,0:T(8,128)(2,1)S(1)}, bf16[2,1,16,2048]{3,2,1,0:T(8,128)(2,1)S(1)}, u32[]{:S(2)}, u32[]{:S(2)}) %collective-permute-start.2) | collective-permute-done | bytes 131104 | tf_op jit(solution)/shard_map/ppermute | solution.py:57
  47.9 0.7 reshape.79
  48.5 0.3 copy.68
  48.8 0.1 pad.2.clone
  49.0 0.2 copy.45
  49.2 0.1 slice.43
  49.3 0.3 copy-done.7
  49.6 3.3 %add_divide_fusion = (f32[3,16,8,5,64]{4,2,3,1,0:T(8,128)}, f32[3,16,8,5,64]{4,2,3,1,0:T(8,128)}, f32[3,16,8,5,64]{4,2,3,1,0:T(8,128)S(1)}) fusion(bf16[3,3,3,64,64]{4,3,2,1,0:T(8,128)(2,1)S(1)} %bitcast.69, bf16[5,16,1,7,2,64]{5,3,4,1,0,2:T(8,128)(2,1)S(1)} %slice.43, bf16[5,16,1,8,5,64]{5,3,4,1,0,2:T(8,128)(2,1)S(1)} %copy.45, pred[8,5]{0,1:T(8,128)(4,1)S(1)} %copy-done.7), kind=kOutput, calls=%fused_computation.15 | convolution fusion | flops 409559040 | bytes 2248744 | tf_op jit(solution)/shard_map/conv_general_dilated | solution.py:81
  52.9 0.2 copy.49
  53.1 2.7 %reshape.99 = bf16[1,5,16,32,64]{4,0,3,2,1:T(2,128)(2,1)} reshape(bf16[1,5,16,2048]{3,2,1,0:T(8,128)(2,1)S(1)} %constant_dynamic-update-slice_fusion.2) | data formatting | bytes 655360 | tf_op jit(solution)/shard_map/reshape | solution.py:80
  55.9 0.3 copy.50
  56.2 0.2 add_divide_fusion.1
  56.4 0.1 copy.47
  56.5 0.1 copy.48
  56.6 0.4 copy-done.5
  57.0 0.3 reshape.78
  57.3 0.1 fusion.23
  57.4 1.2 copy-done
  58.7 3.9 %fusion.2 = bf16[3,3,3,64,64]{4,3,2,1,0:T(8,128)(2,1)S(1)} fusion(bf16[1,5,16,32,64]{4,0,3,2,1:T(2,128)(2,1)S(1)} %copy-done, bf16[1,1,16,32,64]{4,3,2,1,0:T(8,128)(2,1)S(1)} %bitcast.71), kind=kOutput, calls=%fused_computation.6 | convolution fusion | flops 106487808 | bytes 614400 | tf_op jit(solution)/shard_map/transpose | solution.py:110
  62.5 1.0 copy.63
  63.5 1.1 convert_element_type.51
  64.6 16.0 %all-to-all-start = ((bf16[16,1728,4]{1,2,0:T(4,128)(2,1)}), bf16[16,1728,4]{1,2,0:T(4,128)(2,1)S(1)}, u32[]{:S(2)}, u32[]{:S(2)}) async-start(bf16[16,1728,4]{1,2,0:T(4,128)(2,1)} %bitcast.16), calls=%async_computation | async-start | bytes 458752 | tf_op jit(solution)/shard_map/all_to_all | solution.py:30
  80.6 0.3 reshape.77
  80.9 0.2 copy.51
  81.2 1.0 copy-done.1
  82.1 0.2 copy.53
  82.3 0.5 fusion.20
  82.9 0.2 copy.69
  83.0 0.1 pad.4.clone
  83.1 0.1 copy.57
  83.3 0.1 slice.52
  83.3 14.5 %all-to-all-done = bf16[16,1728,4]{1,2,0:T(4,128)(2,1)S(1)} async-done(((bf16[16,1728,4]{1,2,0:T(4,128)(2,1)}), bf16[16,1728,4]{1,2,0:T(4,128)(2,1)S(1)}, u32[]{:S(2)}, u32[]{:S(2)}) %all-to-all-start) | async-done | bytes 221216 | tf_op jit(solution)/shard_map/all_to_all | solution.py:30
  97.8 0.1 convert_reduce_fusion
  97.9 0.2 reshape.56
  98.1 0.7 copy.64
  98.8 14.9 %all-to-all-start.1 = ((f32[64,27,4]{1,2,0:T(4,128)}), f32[64,27,4]{1,2,0:T(4,128)S(1)}, u32[]{:S(2)}, u32[]{:S(2)}) async-start(f32[64,27,4]{1,2,0:T(4,128)} %copy.64), calls=%async_computation.1 | async-start | bytes 262144 | tf_op jit(solution)/shard_map/all_to_all | solution.py:36
  113.8 1.3 fusion.3
  115.2 0.8 reshape.54
  116.0 0.8 reshape.53
  116.8 11.5 %all-to-all-done.1 = f32[64,27,4]{1,2,0:T(4,128)S(1)} async-done(((f32[64,27,4]{1,2,0:T(4,128)}), f32[64,27,4]{1,2,0:T(4,128)S(1)}, u32[]{:S(2)}, u32[]{:S(2)}) %all-to-all-start.1) | async-done | bytes 27680 | tf_op jit(solution)/shard_map/all_to_all | solution.py:36
  128.3 0.7 reduce_sum.19
  (29 shorter events, 0.4 us)
Async XLA Ops:
  0.6 28.8 %copy-start.6 = (bf16[1,1,16,2048]{3,2,1,0:T(8,128)(2,1)S(1)}, bf16[1,1,16,2048]{3,2,1,0:T(8,128)(2,1)}, u32[]{:S(2)}) copy-start(bf16[1,1,16,2048]{3,2,1,0:T(8,128)(2,1)} %param.3) | copy-start | bytes 196612
  0.6 28.8 %collective-permute-start = (bf16[1,1,16,2048]{3,2,1,0:T(8,128)(2,1)}, bf16[1,1,16,2048]{3,2,1,0:T(8,128)(2,1)S(1)}, u32[]{:S(2)}, u32[]{:S(2)}) collective-permute-start(bf16[1,1,16,2048]{3,2,1,0:T(8,128)(2,1)} %param.3), channel_id=1, source_target_pairs={{0,128},{64,192},{128,256},{192,320},{256,384},{320,448},{384,512}... | collective-permute-start | bytes 196616 | tf_op jit(solution)/shard_map/ppermute | solution.py:56
  6.5 22.9 %collective-permute-start.1 = (bf16[2,1,16,2048]{3,2,1,0:T(8,128)(2,1)S(1)}, bf16[2,1,16,2048]{3,2,1,0:T(8,128)(2,1)S(1)}, u32[]{:S(2)}, u32[]{:S(2)}) collective-permute-start(bf16[2,1,16,2048]{3,2,1,0:T(8,128)(2,1)S(1)} %constant_dynamic-update-slice_fusion), channel_id=1, source_target_pairs={{0,64},{64,128},{128,192},{192,256},{256,320},{320,384},{384,448},... | collective-permute-start | bytes 393224 | tf_op jit(solution)/shard_map/ppermute | solution.py:56
  25.6 22.2 %collective-permute-start.2 = (bf16[2,1,16,2048]{3,2,1,0:T(8,128)(2,1)S(1)}, bf16[2,1,16,2048]{3,2,1,0:T(8,128)(2,1)S(1)}, u32[]{:S(2)}, u32[]{:S(2)}) collective-permute-start(bf16[2,1,16,2048]{3,2,1,0:T(8,128)(2,1)S(1)} %constant_dynamic-update-slice_fusion), channel_id=1, source_target_pairs={{64,0},{128,64},{192,128},{256,192},{320,256},{384,320},{448,384},... | collective-permute-start | bytes 393224 | tf_op jit(solution)/shard_map/ppermute | solution.py:57
  26.9 21.0 %collective-permute-start.3 = (bf16[1,1,16,2048]{3,2,1,0:T(8,128)(2,1)}, bf16[1,1,16,2048]{3,2,1,0:T(8,128)(2,1)S(1)}, u32[]{:S(2)}, u32[]{:S(2)}) collective-permute-start(bf16[1,1,16,2048]{3,2,1,0:T(8,128)(2,1)} %param.3), channel_id=1, source_target_pairs={{128,0},{192,64},{256,128},{320,192},{384,256},{448,320},{512,384}... | collective-permute-start | bytes 196616 | tf_op jit(solution)/shard_map/ppermute | solution.py:57
  29.4 19.9 %copy-start.3 = (bf16[1728,64]{1,0:T(8,128)(2,1)}, bf16[1728,64]{1,0:T(8,128)(2,1)S(1)}, u32[]{:S(2)}) copy-start(bf16[1728,64]{1,0:T(8,128)(2,1)S(1)} %copy.65) | copy-start | bytes 663556
  49.0 0.7 copy-start.7
  56.1 0.8 copy-start.5
  57.3 1.3 %copy-start = (bf16[1,5,16,32,64]{4,0,3,2,1:T(2,128)(2,1)S(1)}, bf16[1,5,16,32,64]{4,0,3,2,1:T(2,128)(2,1)}, u32[]{:S(2)}) copy-start(bf16[1,5,16,32,64]{4,0,3,2,1:T(2,128)(2,1)} %reshape.99) | copy-start | bytes 983044
  63.5 17.4 %copy-start.2 = (f32[3,16,8,5,64]{4,2,3,1,0:T(8,128)S(1)}, f32[3,16,8,5,64]{4,2,3,1,0:T(8,128)}, u32[]{:S(2)}) copy-start(f32[3,16,8,5,64]{4,2,3,1,0:T(8,128)} %get-tuple-element.3) | copy-start | bytes 1474564
  64.6 33.3 %all-to-all-start = ((bf16[16,1728,4]{1,2,0:T(4,128)(2,1)}), bf16[16,1728,4]{1,2,0:T(4,128)(2,1)S(1)}, u32[]{:S(2)}, u32[]{:S(2)}) async-start(bf16[16,1728,4]{1,2,0:T(4,128)(2,1)} %bitcast.16), calls=%async_computation | async-start | bytes 458752 | tf_op jit(solution)/shard_map/all_to_all | solution.py:30
  80.9 1.2 copy-start.1
  83.1 30.6 %copy-start.4 = (bf16[1728,64]{1,0:T(8,128)(2,1)S(1)}, bf16[1728,64]{1,0:T(8,128)(2,1)}, u32[]{:S(2)}) copy-start(bf16[1728,64]{1,0:T(8,128)(2,1)} %copy-done.3) | copy-start | bytes 663556
  98.8 29.5 %all-to-all-start.1 = ((f32[64,27,4]{1,2,0:T(4,128)}), f32[64,27,4]{1,2,0:T(4,128)S(1)}, u32[]{:S(2)}, u32[]{:S(2)}) async-start(f32[64,27,4]{1,2,0:T(4,128)} %copy.64), calls=%async_computation.1 | async-start | bytes 262144 | tf_op jit(solution)/shard_map/all_to_all | solution.py:36

commit v4 on v2

--- a/solution.py
+++ b/solution.py
@@ -83,8 +83,12 @@
     )
     scale = 1.0 / math.sqrt(lax.axis_size("dp") * lax.axis_size("gz") * cells)
     terms = grads.transpose(1, 2, 3, 0, 4).reshape(27 * chans, chans) * scale
-    reduced = sum_at_owner(terms.astype(jnp.bfloat16), "dp", 1)
-    weight_grad = sum_at_owner_2(reduced, "gz", 0)
+    gsz, dsz = lax.axis_size("gz"), lax.axis_size("dp")
+    rows, cols = terms.shape
+    arranged = terms.astype(jnp.bfloat16).reshape(gsz, rows // gsz, dsz, cols // dsz)
+    arranged = arranged.transpose(0, 2, 1, 3).reshape(gsz * dsz, rows // gsz, cols // dsz)
+    arrived = lax.all_to_all(arranged, ("gz", "dp"), 0, 0, tiled=True)
+    weight_grad = jnp.sum(arrived.astype(jnp.float32), axis=0)
     return (activation, input_grad, weight_grad)
 
 

time: 119 us -> 145 us (1.22)
  the two profiles are of different devices: /device:TPU:32 before, /device:TPU:1 now
where the time goes in v4:
time: 145 us; the launch traced here: 144 us
  starting transfers between devices  63.2 us (44%)
  waiting for transfers between devices  59.7 us (41%)
  local copies, waits for them, and re-layouts  13.4 us (9%)
  matrix products  5.83 us (4%)
    ppermute x2, waiting for transfers between devices, padded_2(): lax.ppermute(lax.slice_in_dim(block, 0, width, axis=dim), axis, backward)  51.4 us
    ppermute x2, starting transfers between devices, padded_2(): lax.ppermute(lax.slice_in_dim(block, block.shape[dim] - width, None, axis...  36.8 us
    all_to_all x1, starting transfers between devices, per_device(): arrived = lax.all_to_all(arranged, ('gz', 'dp'), 0, 0, tiled=True)  23.8 us
    all_to_all x1, waiting for transfers between devices, per_device(): arrived = lax.all_to_all(arranged, ('gz', 'dp'), 0, 0, tiled=True)  8.31 us
    convert_element_type x2, local copies, waits for them, and re-layouts, per_device(): terms.astype(jnp.bfloat16).reshape(gsz, rows // gsz, dsz, cols // dsz)  4.01 us
    transpose x1, matrix products, per_device(): terms = grads.transpose(1, 2, 3, 0, 4).reshape(27 * chans, chans) * scale  3.72 us
  transfers between devices with their start and end apart: 5, of which 3 were waited for; matrix products, arithmetic and copies ran while one was open for 4% of the time, Pallas kernels for 0%

profile of v4, /device:TPU:1, one launch (start us, length us, event | category | flops | bytes accessed | tf_op | source)
XLA Modules:
  0.0 144.2 jit_solution(3597887715094981093)
XLA Ops:
  0.6 0.0 copy-start.1
  0.6 20.0 %collective-permute-start = (bf16[1,1,16,2048]{3,2,1,0:T(8,128)(2,1)}, bf16[1,1,16,2048]{3,2,1,0:T(8,128)(2,1)S(1)}, u32[]{:S(2)}, u32[]{:S(2)}) collective-permute-start(bf16[1,1,16,2048]{3,2,1,0:T(8,128)(2,1)} %param.3), channel_id=1, source_target_pairs={{0,64},{64,128},{128,192},{192,256},{256,320},{320,384},{384,448},... | collective-permute-start | bytes 196616 | tf_op jit(solution)/shard_map/ppermute | solution.py:14
  20.7 1.3 collective-permute-start.1
  22.0 1.2 copy.112
  23.2 1.0 reshape.123
  24.2 0.0 collective-permute-done
  24.2 0.0 copy-done.1
  24.3 13.2 %collective-permute-done.1 = bf16[1,1,16,2048]{3,2,1,0:T(8,128)(2,1)S(1)} collective-permute-done((bf16[1,1,16,2048]{3,2,1,0:T(8,128)(2,1)}, bf16[1,1,16,2048]{3,2,1,0:T(8,128)(2,1)S(1)}, u32[]{:S(2)}, u32[]{:S(2)}) %collective-permute-start.1) | collective-permute-done | bytes 65568 | tf_op jit(solution)/shard_map/ppermute | solution.py:17
  37.4 0.4 reshape.124
  37.8 0.6 reshape.141
  38.4 0.2 copy.117
  38.5 0.0 copy-start.2
  38.5 0.1 pad.2.clone
  38.6 0.1 copy.91
  38.8 0.1 slice.6
  38.8 0.4 copy-done.2
  39.2 0.8 add_divide_fusion
  40.0 0.1 copy.93
  40.1 0.1 copy.94
  40.2 0.1 reshape.102
  40.4 0.1 copy.103
  40.4 0.1 copy.101
  40.5 0.2 fusion.19
  40.7 3.7 %fusion.2 = bf16[3,3,3,64,64]{4,3,2,1,0:T(8,128)(2,1)S(1)} fusion(bf16[1,3,16,32,64]{4,0,3,2,1:T(2,128)(2,1)S(1)} %reshape.141, bf16[1,1,16,32,64]{4,3,2,1,0:T(8,128)(2,1)S(1)} %fusion.19), kind=kOutput, calls=%fused_computation.4 | convolution fusion | flops 106487808 | bytes 483328 | tf_op jit(solution)/shard_map/transpose | solution.py:85
  44.5 1.0 copy.107
  45.4 3.1 %convert_element_type.56 = bf16[64,27,16,4]{1,0,3,2:T(8,128)(2,1)S(1)} reshape(bf16[3,3,3,64,64]{3,2,1,0,4:T(4,128)(2,1)S(1)} %copy.107) | data formatting | bytes 442368 | tf_op jit(solution)/shard_map/convert_element_type | solution.py:88
  48.5 1.8 %copy.113 = bf16[64,16,27,4]{2,3,1,0:T(4,128)(2,1)} copy(bf16[64,16,27,4]{2,0,3,1:T(8,128)(2,1)S(1)} %bitcast.56) | data formatting | bytes 442368 | tf_op jit(solution)/shard_map/reshape | solution.py:89
  50.3 23.8 %all-to-all-start = ((bf16[1024,27,4]{1,2,0:T(4,128)(2,1)}), bf16[1024,27,4]{1,2,0:T(4,128)(2,1)S(1)}, u32[]{:S(2)}, u32[]{:S(2)}) async-start(bf16[1024,27,4]{1,2,0:T(4,128)(2,1)} %bitcast.13), calls=%async_computation | async-start | bytes 2097152 | tf_op jit(solution)/shard_map/all_to_all | solution.py:90
  74.1 0.0 copy-done
  74.1 0.7 multiply_convert_fusion
  74.8 1.3 collective-permute-start.3
  76.1 16.8 %collective-permute-start.2 = (bf16[1,1,16,2048]{3,2,1,0:T(8,128)(2,1)S(1)}, bf16[1,1,16,2048]{3,2,1,0:T(8,128)(2,1)S(1)}, u32[]{:S(2)}, u32[]{:S(2)}) collective-permute-start(bf16[1,1,16,2048]{3,2,1,0:T(8,128)(2,1)S(1)} %get-tuple-element.14), channel_id=1, source_target_pairs={{0,64},{64,128},{128,192},{192,256},{256,320},{320,384},{384,448},... | collective-permute-start | bytes 196616 | tf_op jit(solution)/shard_map/ppermute | solution.py:14
  92.8 0.2 concatenate.15
  93.0 38.3 %collective-permute-done.3 = bf16[1,1,16,2048]{3,2,1,0:T(8,128)(2,1)S(1)} collective-permute-done((bf16[1,1,16,2048]{3,2,1,0:T(8,128)(2,1)S(1)}, bf16[1,1,16,2048]{3,2,1,0:T(8,128)(2,1)S(1)}, u32[]{:S(2)}, u32[]{:S(2)}) %collective-permute-start.3) | collective-permute-done | bytes 65568 | tf_op jit(solution)/shard_map/ppermute | solution.py:17
  131.3 0.2 concatenate.16
  131.5 0.0 collective-permute-done.2
  131.5 0.2 concatenate.14
  131.6 0.1 maximum_bitcast_fusion
  131.8 0.2 copy.118
  131.9 0.1 pad.4.clone
  132.0 0.1 copy.97
  132.1 0.1 slice.8
  132.2 1.3 fusion.3
  133.6 0.8 reshape.103
  134.4 8.3 %all-to-all-done = bf16[1024,27,4]{1,2,0:T(4,128)(2,1)S(1)} async-done(((bf16[1024,27,4]{1,2,0:T(4,128)(2,1)}), bf16[1024,27,4]{1,2,0:T(4,128)(2,1)S(1)}, u32[]{:S(2)}, u32[]{:S(2)}) %all-to-all-start) | async-done | bytes 221216 | tf_op jit(solution)/shard_map/all_to_all | solution.py:90
  142.7 0.7 copy.110
  143.4 0.2 convert_reduce_fusion
  143.6 0.7 copy.111
  (10 shorter events, 0.1 us)
Async XLA Ops:
  0.6 23.6 %copy-start.1 = (bf16[1,1,16,2048]{3,2,1,0:T(8,128)(2,1)S(1)}, bf16[1,1,16,2048]{3,2,1,0:T(8,128)(2,1)}, u32[]{:S(2)}) copy-start(bf16[1,1,16,2048]{3,2,1,0:T(8,128)(2,1)} %param.3) | copy-start | bytes 196612
  0.6 23.6 %collective-permute-start = (bf16[1,1,16,2048]{3,2,1,0:T(8,128)(2,1)}, bf16[1,1,16,2048]{3,2,1,0:T(8,128)(2,1)S(1)}, u32[]{:S(2)}, u32[]{:S(2)}) collective-permute-start(bf16[1,1,16,2048]{3,2,1,0:T(8,128)(2,1)} %param.3), channel_id=1, source_target_pairs={{0,64},{64,128},{128,192},{192,256},{256,320},{320,384},{384,448},... | collective-permute-start | bytes 196616 | tf_op jit(solution)/shard_map/ppermute | solution.py:14
  20.7 16.7 %collective-permute-start.1 = (bf16[1,1,16,2048]{3,2,1,0:T(8,128)(2,1)}, bf16[1,1,16,2048]{3,2,1,0:T(8,128)(2,1)S(1)}, u32[]{:S(2)}, u32[]{:S(2)}) collective-permute-start(bf16[1,1,16,2048]{3,2,1,0:T(8,128)(2,1)} %param.3), channel_id=1, source_target_pairs={{64,0},{128,64},{192,128},{256,192},{320,256},{384,320},{448,384},... | collective-permute-start | bytes 196616 | tf_op jit(solution)/shard_map/ppermute | solution.py:17
  38.5 0.7 copy-start.2
  50.3 23.8 %copy-start = (bf16[1,1,16,2048]{3,2,1,0:T(8,128)(2,1)S(1)}, bf16[1,1,16,2048]{3,2,1,0:T(8,128)(2,1)}, u32[]{:S(2)}) copy-start(bf16[1,1,16,2048]{3,2,1,0:T(8,128)(2,1)} %param.5) | copy-start | bytes 196612
  50.3 92.4 %all-to-all-start = ((bf16[1024,27,4]{1,2,0:T(4,128)(2,1)}), bf16[1024,27,4]{1,2,0:T(4,128)(2,1)S(1)}, u32[]{:S(2)}, u32[]{:S(2)}) async-start(bf16[1024,27,4]{1,2,0:T(4,128)(2,1)} %bitcast.13), calls=%async_computation | async-start | bytes 2097152 | tf_op jit(solution)/shard_map/all_to_all | solution.py:90
  74.8 56.5 %collective-permute-start.3 = (bf16[1,1,16,2048]{3,2,1,0:T(8,128)(2,1)S(1)}, bf16[1,1,16,2048]{3,2,1,0:T(8,128)(2,1)S(1)}, u32[]{:S(2)}, u32[]{:S(2)}) collective-permute-start(bf16[1,1,16,2048]{3,2,1,0:T(8,128)(2,1)S(1)} %get-tuple-element.14), channel_id=1, source_target_pairs={{64,0},{128,64},{192,128},{256,192},{320,256},{384,320},{448,384},... | collective-permute-start | bytes 196616 | tf_op jit(solution)/shard_map/ppermute | solution.py:17
  76.1 55.4 %collective-permute-start.2 = (bf16[1,1,16,2048]{3,2,1,0:T(8,128)(2,1)S(1)}, bf16[1,1,16,2048]{3,2,1,0:T(8,128)(2,1)S(1)}, u32[]{:S(2)}, u32[]{:S(2)}) collective-permute-start(bf16[1,1,16,2048]{3,2,1,0:T(8,128)(2,1)S(1)} %get-tuple-element.14), channel_id=1, source_target_pairs={{0,64},{64,128},{128,192},{192,256},{256,320},{320,384},{384,448},... | collective-permute-start | bytes 196616 | tf_op jit(solution)/shard_map/ppermute | solution.py:14

commit v5 on v2

--- a/solution.py
+++ b/solution.py
@@ -83,8 +83,8 @@
     )
     scale = 1.0 / math.sqrt(lax.axis_size("dp") * lax.axis_size("gz") * cells)
     terms = grads.transpose(1, 2, 3, 0, 4).reshape(27 * chans, chans) * scale
-    reduced = sum_at_owner(terms.astype(jnp.bfloat16), "dp", 1)
-    weight_grad = sum_at_owner_2(reduced, "gz", 0)
+    reduced = sum_at_owner(terms.astype(jnp.bfloat16), "gz", 0)
+    weight_grad = sum_at_owner_2(reduced, "dp", 1)
     return (activation, input_grad, weight_grad)
 
 

time: 119 us -> 118 us (level)
  the two profiles are of different devices: /device:TPU:32 before, /device:TPU:70 now
where the time goes in v5:
time: 118 us; the launch traced here: 117 us
  starting transfers between devices  70.7 us (60%)
  waiting for transfers between devices  28.9 us (24%)
  local copies, waits for them, and re-layouts  9.32 us (8%)
  matrix products  5.84 us (5%)
  other arithmetic  1.73 us (1%)
    ppermute x2, starting transfers between devices, padded_2(): lax.ppermute(lax.slice_in_dim(block, block.shape[dim] - width, None, axis...  31.9 us
    all_to_all x1, starting transfers between devices, sum_at_owner_2(): lax.all_to_all(pieces, axis, split_axis=0, concat_axis=0, tiled=True)  24.3 us
    all_to_all x1, waiting for transfers between devices, sum_at_owner_2(): lax.all_to_all(pieces, axis, split_axis=0, concat_axis=0, tiled=True)  15.1 us
    ppermute x2, waiting for transfers between devices, padded_2(): lax.ppermute(lax.slice_in_dim(block, 0, width, axis=dim), axis, backward)  12.8 us
    all_to_all x1, starting transfers between devices, sum_at_owner(): pieces = lax.all_to_all(split_up(value, dim, size), axis, 0, 0, tiled=True)  12 us
    transpose x1, matrix products, per_device(): terms = grads.transpose(1, 2, 3, 0, 4).reshape(27 * chans, chans) * scale  3.73 us
    unnamed x12, local copies, waits for them, and re-layouts  2.95 us
    ppermute x2, starting transfers between devices, padded_2(): lax.ppermute(lax.slice_in_dim(block, 0, width, axis=dim), axis, backward)  2.57 us
  transfers between devices with their start and end apart: 6, of which 4 were waited for; matrix products, arithmetic and copies ran while one was open for 5% of the time, Pallas kernels for 0%

profile of v5, /device:TPU:70, one launch (start us, length us, event | category | flops | bytes accessed | tf_op | source)
XLA Modules:
  0.0 117.5 jit_solution(7554962574359118206)
XLA Ops:
  0.6 18.6 %collective-permute-start = (bf16[1,1,16,2048]{3,2,1,0:T(8,128)(2,1)}, bf16[1,1,16,2048]{3,2,1,0:T(8,128)(2,1)S(1)}, u32[]{:S(2)}, u32[]{:S(2)}) collective-permute-start(bf16[1,1,16,2048]{3,2,1,0:T(8,128)(2,1)} %param.3), channel_id=1, source_target_pairs={{0,64},{64,128},{128,192},{192,256},{256,320},{320,384},{384,448},... | collective-permute-start | bytes 196616 | tf_op jit(solution)/shard_map/ppermute | solution.py:14
  19.2 1.3 %collective-permute-start.1 = (bf16[1,1,16,2048]{3,2,1,0:T(8,128)(2,1)}, bf16[1,1,16,2048]{3,2,1,0:T(8,128)(2,1)S(1)}, u32[]{:S(2)}, u32[]{:S(2)}) collective-permute-start(bf16[1,1,16,2048]{3,2,1,0:T(8,128)(2,1)} %param.3), channel_id=1, source_target_pairs={{64,0},{128,64},{192,128},{256,192},{320,256},{384,320},{448,384},... | collective-permute-start | bytes 196616 | tf_op jit(solution)/shard_map/ppermute | solution.py:17
  20.5 1.2 %copy.58 = bf16[1728,64]{1,0:T(8,128)(2,1)S(1)} copy(bf16[1728,64]{0,1:T(8,128)(2,1)} %param.4) | data formatting | bytes 442368 | tf_op jit(solution)/shard_map/reshape | solution.py:55
  21.7 1.0 reshape.123
  22.8 0.0 collective-permute-done
  22.8 12.2 %collective-permute-done.1 = bf16[1,1,16,2048]{3,2,1,0:T(8,128)(2,1)S(1)} collective-permute-done((bf16[1,1,16,2048]{3,2,1,0:T(8,128)(2,1)}, bf16[1,1,16,2048]{3,2,1,0:T(8,128)(2,1)S(1)}, u32[]{:S(2)}, u32[]{:S(2)}) %collective-permute-start.1) | collective-permute-done | bytes 65568 | tf_op jit(solution)/shard_map/ppermute | solution.py:17
  35.0 0.4 reshape.124
  35.4 0.6 reshape.141
  36.0 0.2 copy.61
  36.1 0.1 pad.2.clone
  36.2 0.0 copy-start.2
  36.2 0.1 copy.41
  36.4 0.1 slice.6
  36.4 0.5 copy-done.2
  36.9 0.8 add_divide_fusion
  37.7 0.1 copy.53
  37.8 0.1 copy.51
  37.9 0.2 fusion.19
  38.1 3.7 %fusion.2 = bf16[3,3,3,64,64]{4,3,2,1,0:T(8,128)(2,1)S(1)} fusion(bf16[1,3,16,32,64]{4,0,3,2,1:T(2,128)(2,1)S(1)} %reshape.141, bf16[1,1,16,32,64]{4,3,2,1,0:T(8,128)(2,1)S(1)} %fusion.19), kind=kOutput, calls=%fused_computation.4 | convolution fusion | flops 106487808 | bytes 483328 | tf_op jit(solution)/shard_map/transpose | solution.py:85
  41.9 0.1 convert_element_type.56
  42.0 1.1 reshape.142
  43.1 12.0 %all-to-all-start = ((bf16[64,2,864]{2,1,0:T(2,128)(2,1)}), bf16[64,2,864]{2,1,0:T(2,128)(2,1)S(1)}, u32[]{:S(2)}, u32[]{:S(2)}) async-start(bf16[64,2,864]{2,1,0:T(2,128)(2,1)} %reshape.142), calls=%async_computation | async-start | bytes 458752 | tf_op jit(solution)/shard_map/all_to_all | solution.py:30
  55.2 0.1 copy.43
  55.2 0.0 copy-start
  55.3 0.1 copy.44
  55.4 0.1 reshape.102
  55.5 0.6 copy-done
  56.1 0.7 multiply_convert_fusion
  56.8 1.3 %collective-permute-start.3 = (bf16[1,1,16,2048]{3,2,1,0:T(8,128)(2,1)S(1)}, bf16[1,1,16,2048]{3,2,1,0:T(8,128)(2,1)S(1)}, u32[]{:S(2)}, u32[]{:S(2)}) collective-permute-start(bf16[1,1,16,2048]{3,2,1,0:T(8,128)(2,1)S(1)} %get-tuple-element.5), channel_id=1, source_target_pairs={{64,0},{128,64},{192,128},{256,192},{320,256},{384,320},{448,384},... | collective-permute-start | bytes 196616 | tf_op jit(solution)/shard_map/ppermute | solution.py:17
  58.1 13.3 %collective-permute-start.2 = (bf16[1,1,16,2048]{3,2,1,0:T(8,128)(2,1)S(1)}, bf16[1,1,16,2048]{3,2,1,0:T(8,128)(2,1)S(1)}, u32[]{:S(2)}, u32[]{:S(2)}) collective-permute-start(bf16[1,1,16,2048]{3,2,1,0:T(8,128)(2,1)S(1)} %get-tuple-element.5), channel_id=1, source_target_pairs={{0,64},{64,128},{128,192},{192,256},{256,320},{320,384},{384,448},... | collective-permute-start | bytes 196616 | tf_op jit(solution)/shard_map/ppermute | solution.py:14
  71.3 0.2 concatenate.15
  71.5 0.6 collective-permute-done.3
  72.1 0.2 concatenate.16
  72.3 0.9 collective-permute-done.2
  73.2 0.2 concatenate.14
  73.4 0.1 maximum_bitcast_fusion
  73.5 0.2 copy.62
  73.7 0.1 pad.4.clone
  73.8 0.1 copy.47
  73.9 0.1 slice.8
  74.0 0.4 reshape.143
  74.4 0.1 convert_reduce_fusion
  74.6 0.7 copy.57
  75.2 24.3 %all-to-all-start.1 = ((f32[16,27,4]{1,2,0:T(4,128)}), f32[16,27,4]{1,2,0:T(4,128)S(1)}, u32[]{:S(2)}, u32[]{:S(2)}) async-start(f32[16,27,4]{1,2,0:T(4,128)} %bitcast.13), calls=%async_computation.1 | async-start | bytes 65536 | tf_op jit(solution)/shard_map/all_to_all | solution.py:36
  99.5 1.3 %fusion.3 = bf16[1,16,8,5,64]{4,2,3,1,0:T(8,128)(2,1)S(1)} fusion(bf16[3,3,3,64,64]{4,3,2,1,0:T(8,128)(2,1)S(1)} %bitcast.64, bf16[3,16,1,7,2,64]{5,3,4,1,0,2:T(8,128)(2,1)S(1)} %slice.8, bf16[3,16,1,8,5,64]{5,3,4,1,0,2:T(8,128)(2,1)S(1)} %copy.47, pred[8,5]{0,1:T(8,128)(4,1)S(1)} %copy-done.2), kind=kOutput, calls=%fused_computation.7 | convolution fusion | flops 136773632 | bytes 634920 | tf_op jit(solution)/shard_map/conv_general_dilated | solution.py:71
  100.9 0.8 reshape.103
  101.7 15.1 %all-to-all-done.1 = f32[16,27,4]{1,2,0:T(4,128)S(1)} async-done(((f32[16,27,4]{1,2,0:T(4,128)}), f32[16,27,4]{1,2,0:T(4,128)S(1)}, u32[]{:S(2)}, u32[]{:S(2)}) %all-to-all-start.1) | async-done | bytes 6944 | tf_op jit(solution)/shard_map/all_to_all | solution.py:36
  116.9 0.6 reduce_sum.19
  (12 shorter events, 0.2 us)
Async XLA Ops:
  0.6 22.2 %copy-start.1 = (bf16[1,1,16,2048]{3,2,1,0:T(8,128)(2,1)S(1)}, bf16[1,1,16,2048]{3,2,1,0:T(8,128)(2,1)}, u32[]{:S(2)}) copy-start(bf16[1,1,16,2048]{3,2,1,0:T(8,128)(2,1)} %param.3) | copy-start | bytes 196612
  0.6 22.1 %collective-permute-start = (bf16[1,1,16,2048]{3,2,1,0:T(8,128)(2,1)}, bf16[1,1,16,2048]{3,2,1,0:T(8,128)(2,1)S(1)}, u32[]{:S(2)}, u32[]{:S(2)}) collective-permute-start(bf16[1,1,16,2048]{3,2,1,0:T(8,128)(2,1)} %param.3), channel_id=1, source_target_pairs={{0,64},{64,128},{128,192},{192,256},{256,320},{320,384},{384,448},... | collective-permute-start | bytes 196616 | tf_op jit(solution)/shard_map/ppermute | solution.py:14
  19.2 15.8 %collective-permute-start.1 = (bf16[1,1,16,2048]{3,2,1,0:T(8,128)(2,1)}, bf16[1,1,16,2048]{3,2,1,0:T(8,128)(2,1)S(1)}, u32[]{:S(2)}, u32[]{:S(2)}) collective-permute-start(bf16[1,1,16,2048]{3,2,1,0:T(8,128)(2,1)} %param.3), channel_id=1, source_target_pairs={{64,0},{128,64},{192,128},{256,192},{320,256},{384,320},{448,384},... | collective-permute-start | bytes 196616 | tf_op jit(solution)/shard_map/ppermute | solution.py:17
  36.2 0.7 copy-start.2
  43.1 30.8 %all-to-all-start = ((bf16[64,2,864]{2,1,0:T(2,128)(2,1)}), bf16[64,2,864]{2,1,0:T(2,128)(2,1)S(1)}, u32[]{:S(2)}, u32[]{:S(2)}) async-start(bf16[64,2,864]{2,1,0:T(2,128)(2,1)} %reshape.142), calls=%async_computation | async-start | bytes 458752 | tf_op jit(solution)/shard_map/all_to_all | solution.py:30
  55.2 0.8 copy-start
  56.8 15.4 %collective-permute-start.3 = (bf16[1,1,16,2048]{3,2,1,0:T(8,128)(2,1)S(1)}, bf16[1,1,16,2048]{3,2,1,0:T(8,128)(2,1)S(1)}, u32[]{:S(2)}, u32[]{:S(2)}) collective-permute-start(bf16[1,1,16,2048]{3,2,1,0:T(8,128)(2,1)S(1)} %get-tuple-element.5), channel_id=1, source_target_pairs={{64,0},{128,64},{192,128},{256,192},{320,256},{384,320},{448,384},... | collective-permute-start | bytes 196616 | tf_op jit(solution)/shard_map/ppermute | solution.py:17
  58.1 15.2 %collective-permute-start.2 = (bf16[1,1,16,2048]{3,2,1,0:T(8,128)(2,1)S(1)}, bf16[1,1,16,2048]{3,2,1,0:T(8,128)(2,1)S(1)}, u32[]{:S(2)}, u32[]{:S(2)}) collective-permute-start(bf16[1,1,16,2048]{3,2,1,0:T(8,128)(2,1)S(1)} %get-tuple-element.5), channel_id=1, source_target_pairs={{0,64},{64,128},{128,192},{192,256},{256,320},{320,384},{384,448},... | collective-permute-start | bytes 196616 | tf_op jit(solution)/shard_map/ppermute | solution.py:14
  75.2 41.6 %all-to-all-start.1 = ((f32[16,27,4]{1,2,0:T(4,128)}), f32[16,27,4]{1,2,0:T(4,128)S(1)}, u32[]{:S(2)}, u32[]{:S(2)}) async-start(f32[16,27,4]{1,2,0:T(4,128)} %bitcast.13), calls=%async_computation.1 | async-start | bytes 65536 | tf_op jit(solution)/shard_map/all_to_all | solution.py:36

commit v6 on v2

--- a/solution.py
+++ b/solution.py
@@ -65,13 +65,6 @@
     delta = (
         cotangent.reshape(cells, chans).astype(jnp.float32) * sig * (1.0 + pre * (1.0 - sig))
     ).astype(jnp.bfloat16)
-    delta_ext = padded_2(delta.reshape(1, planes, height, width * chans), (("dp", 1),), 1)
-    d_ext = delta_ext.reshape(1, planes + 2, height, width, chans)
-    flipped = jnp.flip(kern, (0, 1, 2)).transpose(0, 1, 2, 4, 3)
-    back = lax.conv_general_dilated(
-        d_ext, flipped, (1, 1, 1), same, dimension_numbers=dims, preferred_element_type=jnp.float32
-    )
-    input_grad = back.astype(jnp.bfloat16).reshape(1, planes, height, width * chans)
     v_pad = jnp.pad(v_ext, ((0, 0), (0, 0), (1, 1), (1, 1), (0, 0)))
     grads = lax.conv_general_dilated(
         v_pad,
@@ -85,6 +78,14 @@
     terms = grads.transpose(1, 2, 3, 0, 4).reshape(27 * chans, chans) * scale
     reduced = sum_at_owner(terms.astype(jnp.bfloat16), "dp", 1)
     weight_grad = sum_at_owner_2(reduced, "gz", 0)
+    late, _ = lax.optimization_barrier((delta, reduced))
+    delta_ext = padded_2(late.reshape(1, planes, height, width * chans), (("dp", 1),), 1)
+    d_ext = delta_ext.reshape(1, planes + 2, height, width, chans)
+    flipped = jnp.flip(kern, (0, 1, 2)).transpose(0, 1, 2, 4, 3)
+    back = lax.conv_general_dilated(
+        d_ext, flipped, (1, 1, 1), same, dimension_numbers=dims, preferred_element_type=jnp.float32
+    )
+    input_grad = back.astype(jnp.bfloat16).reshape(1, planes, height, width * chans)
     return (activation, input_grad, weight_grad)
 
 

time: 119 us -> 123 us (1.034)
  the two profiles are of different devices: /device:TPU:32 before, /device:TPU:8 now
where the time goes in v6:
time: 123 us
  starting transfers between devices  63.9 us (52%)
  waiting for transfers between devices  40.7 us (33%)
  local copies, waits for them, and re-layouts  9.46 us (8%)
  matrix products  5.84 us (5%)
  other arithmetic  1.85 us (2%)
    ppermute x2, starting transfers between devices, padded_2(): lax.ppermute(lax.slice_in_dim(block, block.shape[dim] - width, None, axis...  23.4 us
    all_to_all x1, starting transfers between devices, sum_at_owner_2(): lax.all_to_all(pieces, axis, split_axis=0, concat_axis=0, tiled=True)  19.1 us
    all_to_all x1, waiting for transfers between devices, sum_at_owner(): pieces = lax.all_to_all(split_up(value, dim, size), axis, 0, 0, tiled=True)  16.3 us
    ppermute x2, starting transfers between devices, padded_2(): lax.ppermute(lax.slice_in_dim(block, 0, width, axis=dim), axis, backward)  13.5 us
    ppermute x2, waiting for transfers between devices, padded_2(): lax.ppermute(lax.slice_in_dim(block, 0, width, axis=dim), axis, backward)  11.7 us
    all_to_all x1, waiting for transfers between devices, sum_at_owner_2(): lax.all_to_all(pieces, axis, split_axis=0, concat_axis=0, tiled=True)  11.7 us
    all_to_all x1, starting transfers between devices, sum_at_owner(): pieces = lax.all_to_all(split_up(value, dim, size), axis, 0, 0, tiled=True)  7.88 us
    transpose x1, matrix products, per_device(): terms = grads.transpose(1, 2, 3, 0, 4).reshape(27 * chans, chans) * scale  3.73 us
  transfers between devices with their start and end apart: 6, of which 4 were waited for; matrix products, arithmetic and copies ran while one was open for 6% of the time, Pallas kernels for 0%

profile of v6, /device:TPU:8, one launch (start us, length us, event | category | flops | bytes accessed | tf_op | source)
XLA Modules:
  0.0 122.7 jit_solution(14808870431727621296)
XLA Ops:
  0.6 19.5 %collective-permute-start = (bf16[1,1,16,2048]{3,2,1,0:T(8,128)(2,1)}, bf16[1,1,16,2048]{3,2,1,0:T(8,128)(2,1)S(1)}, u32[]{:S(2)}, u32[]{:S(2)}) collective-permute-start(bf16[1,1,16,2048]{3,2,1,0:T(8,128)(2,1)} %param.3), channel_id=1, source_target_pairs={{0,64},{64,128},{128,192},{192,256},{256,320},{320,384},{384,448},... | collective-permute-start | bytes 196616 | tf_op jit(solution)/shard_map/ppermute | solution.py:14
  20.1 1.9 %collective-permute-start.1 = (bf16[1,1,16,2048]{3,2,1,0:T(8,128)(2,1)}, bf16[1,1,16,2048]{3,2,1,0:T(8,128)(2,1)S(1)}, u32[]{:S(2)}, u32[]{:S(2)}) collective-permute-start(bf16[1,1,16,2048]{3,2,1,0:T(8,128)(2,1)} %param.3), channel_id=1, source_target_pairs={{64,0},{128,64},{192,128},{256,192},{320,256},{384,320},{448,384},... | collective-permute-start | bytes 196616 | tf_op jit(solution)/shard_map/ppermute | solution.py:17
  22.1 1.2 copy.70
  23.3 1.0 reshape.111
  24.3 0.9 collective-permute-done
  25.2 11.7 %collective-permute-done.1 = bf16[1,1,16,2048]{3,2,1,0:T(8,128)(2,1)S(1)} collective-permute-done((bf16[1,1,16,2048]{3,2,1,0:T(8,128)(2,1)}, bf16[1,1,16,2048]{3,2,1,0:T(8,128)(2,1)S(1)}, u32[]{:S(2)}, u32[]{:S(2)}) %collective-permute-start.1) | collective-permute-done | bytes 65568 | tf_op jit(solution)/shard_map/ppermute | solution.py:17
  36.9 0.4 reshape.112
  37.3 0.6 reshape.130
  37.9 0.2 copy.73
  38.1 0.1 pad.2.clone
  38.2 0.1 copy.49
  38.3 0.1 slice.6
  38.4 0.5 copy-done.2
  38.8 0.8 add_divide_fusion
  39.7 0.1 copy.54
  39.8 0.1 copy.56
  39.9 0.2 fusion.19
  40.1 3.7 %fusion.2 = bf16[3,3,3,64,64]{4,3,2,1,0:T(8,128)(2,1)S(1)} fusion(bf16[1,3,16,32,64]{4,0,3,2,1:T(2,128)(2,1)S(1)} %reshape.130, bf16[1,1,16,32,64]{4,3,2,1,0:T(8,128)(2,1)S(1)} %fusion.19), kind=kOutput, calls=%fused_computation.4 | convolution fusion | flops 106487808 | bytes 483328 | tf_op jit(solution)/shard_map/transpose | solution.py:78
  43.8 1.0 copy.60
  44.8 1.1 convert_element_type.57
  45.8 7.9 %all-to-all-start = ((bf16[16,1728,4]{1,2,0:T(4,128)(2,1)}), bf16[16,1728,4]{1,2,0:T(4,128)(2,1)S(1)}, u32[]{:S(2)}, u32[]{:S(2)}) async-start(bf16[16,1728,4]{1,2,0:T(4,128)(2,1)} %bitcast.9), calls=%async_computation | async-start | bytes 458752 | tf_op jit(solution)/shard_map/all_to_all | solution.py:30
  53.7 0.2 reshape.110
  53.9 0.1 copy.51
  54.0 0.1 copy.52
  54.1 0.1 reshape.87
  54.2 0.1 fusion.26
  54.3 16.3 %all-to-all-done = bf16[16,1728,4]{1,2,0:T(4,128)(2,1)S(1)} async-done(((bf16[16,1728,4]{1,2,0:T(4,128)(2,1)}), bf16[16,1728,4]{1,2,0:T(4,128)(2,1)S(1)}, u32[]{:S(2)}, u32[]{:S(2)}) %all-to-all-start) | async-done | bytes 221216 | tf_op jit(solution)/shard_map/all_to_all | solution.py:30
  70.7 0.1 convert_reduce_fusion
  70.8 0.2 reshape.89
  71.0 3.9 %collective-permute-start.2 = (bf16[1,1,16,2048]{3,2,1,0:T(8,128)(2,1)S(1)}, bf16[1,1,16,2048]{3,2,1,0:T(8,128)(2,1)S(1)}, u32[]{:S(2)}, u32[]{:S(2)}) collective-permute-start(bf16[1,1,16,2048]{3,2,1,0:T(8,128)(2,1)S(1)} %reshape.89), channel_id=1, source_target_pairs={{0,64},{64,128},{128,192},{192,256},{256,320},{320,384},{384,448},... | collective-permute-start | bytes 196616 | tf_op jit(solution)/shard_map/ppermute | solution.py:14
  74.8 11.6 %collective-permute-start.3 = (bf16[1,1,16,2048]{3,2,1,0:T(8,128)(2,1)S(1)}, bf16[1,1,16,2048]{3,2,1,0:T(8,128)(2,1)S(1)}, u32[]{:S(2)}, u32[]{:S(2)}) collective-permute-start(bf16[1,1,16,2048]{3,2,1,0:T(8,128)(2,1)S(1)} %reshape.89), channel_id=1, source_target_pairs={{64,0},{128,64},{192,128},{256,192},{320,256},{384,320},{448,384},... | collective-permute-start | bytes 196616 | tf_op jit(solution)/shard_map/ppermute | solution.py:17
  86.4 0.7 multiply_convert_fusion
  87.1 0.2 reshape.91
  87.3 0.1 copy.62
  87.3 0.7 copy.69
  88.1 19.1 %all-to-all-start.1 = ((f32[64,27,4]{1,2,0:T(4,128)}), f32[64,27,4]{1,2,0:T(4,128)S(1)}, u32[]{:S(2)}, u32[]{:S(2)}) async-start(f32[64,27,4]{1,2,0:T(4,128)} %copy.69), calls=%async_computation.1 | async-start | bytes 262144 | tf_op jit(solution)/shard_map/all_to_all | solution.py:36
  107.2 0.2 concatenate.14
  107.4 0.1 copy.61
  107.5 0.2 concatenate.16
  107.6 0.1 copy.63
  107.7 0.1 maximum_bitcast_fusion
  107.8 0.1 pad.4
  107.9 0.1 copy.65
  108.0 0.1 slice.10
  108.1 1.3 %fusion.3 = bf16[1,16,8,5,64]{4,2,3,1,0:T(8,128)(2,1)S(1)} fusion(bf16[3,3,3,64,64]{4,3,2,1,0:T(8,128)(2,1)S(1)} %bitcast.83, bf16[3,16,1,7,2,64]{5,3,4,1,0,2:T(8,128)(2,1)S(1)} %slice.10, bf16[3,16,1,8,5,64]{5,3,4,1,0,2:T(8,128)(2,1)S(1)} %copy.65, pred[8,5]{0,1:T(8,128)(4,1)S(1)} %copy-done.2), kind=kOutput, calls=%fused_computation.7 | convolution fusion | flops 136773632 | bytes 634920 | tf_op jit(solution)/shard_map/conv_general_dilated | solution.py:85
  109.5 0.8 reshape.90
  110.3 11.7 %all-to-all-done.1 = f32[64,27,4]{1,2,0:T(4,128)S(1)} async-done(((f32[64,27,4]{1,2,0:T(4,128)}), f32[64,27,4]{1,2,0:T(4,128)S(1)}, u32[]{:S(2)}, u32[]{:S(2)}) %all-to-all-start.1) | async-done | bytes 27680 | tf_op jit(solution)/shard_map/all_to_all | solution.py:36
  122.0 0.7 reduce_sum.19
  (16 shorter events, 0.2 us)
Async XLA Ops:
  0.6 24.6 %copy-start.1 = (bf16[1,1,16,2048]{3,2,1,0:T(8,128)(2,1)S(1)}, bf16[1,1,16,2048]{3,2,1,0:T(8,128)(2,1)}, u32[]{:S(2)}) copy-start(bf16[1,1,16,2048]{3,2,1,0:T(8,128)(2,1)} %param.3) | copy-start | bytes 196612
  0.6 24.6 %collective-permute-start = (bf16[1,1,16,2048]{3,2,1,0:T(8,128)(2,1)}, bf16[1,1,16,2048]{3,2,1,0:T(8,128)(2,1)S(1)}, u32[]{:S(2)}, u32[]{:S(2)}) collective-permute-start(bf16[1,1,16,2048]{3,2,1,0:T(8,128)(2,1)} %param.3), channel_id=1, source_target_pairs={{0,64},{64,128},{128,192},{192,256},{256,320},{320,384},{384,448},... | collective-permute-start | bytes 196616 | tf_op jit(solution)/shard_map/ppermute | solution.py:14
  20.1 16.8 %collective-permute-start.1 = (bf16[1,1,16,2048]{3,2,1,0:T(8,128)(2,1)}, bf16[1,1,16,2048]{3,2,1,0:T(8,128)(2,1)S(1)}, u32[]{:S(2)}, u32[]{:S(2)}) collective-permute-start(bf16[1,1,16,2048]{3,2,1,0:T(8,128)(2,1)} %param.3), channel_id=1, source_target_pairs={{64,0},{128,64},{192,128},{256,192},{320,256},{384,320},{448,384},... | collective-permute-start | bytes 196616 | tf_op jit(solution)/shard_map/ppermute | solution.py:17
  38.2 0.7 copy-start.2
  44.8 9.0 %copy-start = (bf16[1,1,16,2048]{3,2,1,0:T(8,128)(2,1)S(1)}, bf16[1,1,16,2048]{3,2,1,0:T(8,128)(2,1)}, u32[]{:S(2)}) copy-start(bf16[1,1,16,2048]{3,2,1,0:T(8,128)(2,1)} %param.5) | copy-start | bytes 196612
  45.8 24.8 %all-to-all-start = ((bf16[16,1728,4]{1,2,0:T(4,128)(2,1)}), bf16[16,1728,4]{1,2,0:T(4,128)(2,1)S(1)}, u32[]{:S(2)}, u32[]{:S(2)}) async-start(bf16[16,1728,4]{1,2,0:T(4,128)(2,1)} %bitcast.9), calls=%async_computation | async-start | bytes 458752 | tf_op jit(solution)/shard_map/all_to_all | solution.py:30
  71.0 36.3 %collective-permute-start.2 = (bf16[1,1,16,2048]{3,2,1,0:T(8,128)(2,1)S(1)}, bf16[1,1,16,2048]{3,2,1,0:T(8,128)(2,1)S(1)}, u32[]{:S(2)}, u32[]{:S(2)}) collective-permute-start(bf16[1,1,16,2048]{3,2,1,0:T(8,128)(2,1)S(1)} %reshape.89), channel_id=1, source_target_pairs={{0,64},{64,128},{128,192},{192,256},{256,320},{320,384},{384,448},... | collective-permute-start | bytes 196616 | tf_op jit(solution)/shard_map/ppermute | solution.py:14
  74.8 32.6 %collective-permute-start.3 = (bf16[1,1,16,2048]{3,2,1,0:T(8,128)(2,1)S(1)}, bf16[1,1,16,2048]{3,2,1,0:T(8,128)(2,1)S(1)}, u32[]{:S(2)}, u32[]{:S(2)}) collective-permute-start(bf16[1,1,16,2048]{3,2,1,0:T(8,128)(2,1)S(1)} %reshape.89), channel_id=1, source_target_pairs={{64,0},{128,64},{192,128},{256,192},{320,256},{384,320},{448,384},... | collective-permute-start | bytes 196616 | tf_op jit(solution)/shard_map/ppermute | solution.py:17
  88.1 33.9 %all-to-all-start.1 = ((f32[64,27,4]{1,2,0:T(4,128)}), f32[64,27,4]{1,2,0:T(4,128)S(1)}, u32[]{:S(2)}, u32[]{:S(2)}) async-start(f32[64,27,4]{1,2,0:T(4,128)} %copy.69), calls=%async_computation.1 | async-start | bytes 262144 | tf_op jit(solution)/shard_map/all_to_all | solution.py:36

commit v7 on v2

--- a/solution.py
+++ b/solution.py
@@ -84,7 +84,7 @@
     scale = 1.0 / math.sqrt(lax.axis_size("dp") * lax.axis_size("gz") * cells)
     terms = grads.transpose(1, 2, 3, 0, 4).reshape(27 * chans, chans) * scale
     reduced = sum_at_owner(terms.astype(jnp.bfloat16), "dp", 1)
-    weight_grad = sum_at_owner_2(reduced, "gz", 0)
+    weight_grad = sum_at_owner(reduced.astype(jnp.bfloat16), "gz", 0)
     return (activation, input_grad, weight_grad)
 
 

time: 119 us -> 117 us (0.983)
  the two profiles are of different devices: /device:TPU:32 before, /device:TPU:33 now
where the time goes in v7:
time: 117 us; the launch traced here: 116 us
  starting transfers between devices  60.6 us (52%)
  waiting for transfers between devices  37.2 us (32%)
  local copies, waits for them, and re-layouts  9.83 us (8%)
  matrix products  5.84 us (5%)
  other arithmetic  1.75 us (1%)
    all_to_all x2, starting transfers between devices, sum_at_owner(): pieces = lax.all_to_all(split_up(value, dim, size), axis, 0, 0, tiled=True)  25.5 us
    ppermute x2, starting transfers between devices, padded_2(): lax.ppermute(lax.slice_in_dim(block, block.shape[dim] - width, None, axis...  21.4 us
    ppermute x2, waiting for transfers between devices, padded_2(): lax.ppermute(lax.slice_in_dim(block, 0, width, axis=dim), axis, backward)  20 us
    ppermute x2, starting transfers between devices, padded_2(): lax.ppermute(lax.slice_in_dim(block, 0, width, axis=dim), axis, backward)  13.7 us
    all_to_all x2, waiting for transfers between devices, sum_at_owner(): pieces = lax.all_to_all(split_up(value, dim, size), axis, 0, 0, tiled=True)  10.6 us
    ppermute x2, waiting for transfers between devices, padded_2(): lax.ppermute(lax.slice_in_dim(block, block.shape[dim] - width, None, axis...  6.58 us
    transpose x1, matrix products, per_device(): terms = grads.transpose(1, 2, 3, 0, 4).reshape(27 * chans, chans) * scale  3.73 us
  transfers between devices with their start and end apart: 6, of which 4 were waited for; matrix products, arithmetic and copies ran while one was open for 6% of the time, Pallas kernels for 0%

profile of v7, /device:TPU:33, one launch (start us, length us, event | category | flops | bytes accessed | tf_op | source)
XLA Modules:
  0.0 116.2 jit_solution(18340382865065271386)
XLA Ops:
  0.6 19.2 %collective-permute-start = (bf16[1,1,16,2048]{3,2,1,0:T(8,128)(2,1)}, bf16[1,1,16,2048]{3,2,1,0:T(8,128)(2,1)S(1)}, u32[]{:S(2)}, u32[]{:S(2)}) collective-permute-start(bf16[1,1,16,2048]{3,2,1,0:T(8,128)(2,1)} %param.3), channel_id=1, source_target_pairs={{0,64},{64,128},{128,192},{192,256},{256,320},{320,384},{384,448},... | collective-permute-start | bytes 196616 | tf_op jit(solution)/shard_map/ppermute | solution.py:14
  19.9 1.9 %collective-permute-start.1 = (bf16[1,1,16,2048]{3,2,1,0:T(8,128)(2,1)}, bf16[1,1,16,2048]{3,2,1,0:T(8,128)(2,1)S(1)}, u32[]{:S(2)}, u32[]{:S(2)}) collective-permute-start(bf16[1,1,16,2048]{3,2,1,0:T(8,128)(2,1)} %param.3), channel_id=1, source_target_pairs={{64,0},{128,64},{192,128},{256,192},{320,256},{384,320},{448,384},... | collective-permute-start | bytes 196616 | tf_op jit(solution)/shard_map/ppermute | solution.py:17
  21.8 1.2 %copy.61 = bf16[1728,64]{1,0:T(8,128)(2,1)S(1)} copy(bf16[1728,64]{0,1:T(8,128)(2,1)} %param.4) | data formatting | bytes 442368 | tf_op jit(solution)/shard_map/reshape | solution.py:55
  23.0 1.0 reshape.123
  24.0 0.0 collective-permute-done
  24.1 13.0 %collective-permute-done.1 = bf16[1,1,16,2048]{3,2,1,0:T(8,128)(2,1)S(1)} collective-permute-done((bf16[1,1,16,2048]{3,2,1,0:T(8,128)(2,1)}, bf16[1,1,16,2048]{3,2,1,0:T(8,128)(2,1)S(1)}, u32[]{:S(2)}, u32[]{:S(2)}) %collective-permute-start.1) | collective-permute-done | bytes 65568 | tf_op jit(solution)/shard_map/ppermute | solution.py:17
  37.0 0.4 reshape.124
  37.4 0.6 reshape.141
  38.0 0.2 copy.64
  38.1 0.1 pad.2.clone
  38.2 0.0 copy-start.2
  38.2 0.1 copy.43
  38.4 0.1 slice.6
  38.4 0.5 copy-done.2
  38.9 0.8 add_divide_fusion
  39.7 0.1 copy.55
  39.8 0.1 copy.53
  39.9 0.2 fusion.19
  40.1 3.7 %fusion.2 = bf16[3,3,3,64,64]{4,3,2,1,0:T(8,128)(2,1)S(1)} fusion(bf16[1,3,16,32,64]{4,0,3,2,1:T(2,128)(2,1)S(1)} %reshape.141, bf16[1,1,16,32,64]{4,3,2,1,0:T(8,128)(2,1)S(1)} %fusion.19), kind=kOutput, calls=%fused_computation.4 | convolution fusion | flops 106487808 | bytes 483328 | tf_op jit(solution)/shard_map/transpose | solution.py:85
  43.9 1.0 copy.59
  44.8 1.1 convert_element_type.58
  45.9 6.7 %all-to-all-start = ((bf16[16,1728,4]{1,2,0:T(4,128)(2,1)}), bf16[16,1728,4]{1,2,0:T(4,128)(2,1)S(1)}, u32[]{:S(2)}, u32[]{:S(2)}) async-start(bf16[16,1728,4]{1,2,0:T(4,128)(2,1)} %bitcast.12), calls=%async_computation | async-start | bytes 458752 | tf_op jit(solution)/shard_map/all_to_all | solution.py:30
  52.6 0.1 copy.45
  52.7 0.0 copy-start
  52.7 0.1 copy.46
  52.8 0.1 reshape.102
  52.9 0.6 copy-done
  53.5 0.7 multiply_convert_fusion
  54.2 11.8 %collective-permute-start.3 = (bf16[1,1,16,2048]{3,2,1,0:T(8,128)(2,1)S(1)}, bf16[1,1,16,2048]{3,2,1,0:T(8,128)(2,1)S(1)}, u32[]{:S(2)}, u32[]{:S(2)}) collective-permute-start(bf16[1,1,16,2048]{3,2,1,0:T(8,128)(2,1)S(1)} %get-tuple-element.5), channel_id=1, source_target_pairs={{64,0},{128,64},{192,128},{256,192},{320,256},{384,320},{448,384},... | collective-permute-start | bytes 196616 | tf_op jit(solution)/shard_map/ppermute | solution.py:17
  66.0 2.2 %collective-permute-start.2 = (bf16[1,1,16,2048]{3,2,1,0:T(8,128)(2,1)S(1)}, bf16[1,1,16,2048]{3,2,1,0:T(8,128)(2,1)S(1)}, u32[]{:S(2)}, u32[]{:S(2)}) collective-permute-start(bf16[1,1,16,2048]{3,2,1,0:T(8,128)(2,1)S(1)} %get-tuple-element.5), channel_id=1, source_target_pairs={{0,64},{64,128},{128,192},{192,256},{256,320},{320,384},{384,448},... | collective-permute-start | bytes 196616 | tf_op jit(solution)/shard_map/ppermute | solution.py:14
  68.2 0.2 concatenate.15
  68.4 7.1 %collective-permute-done.3 = bf16[1,1,16,2048]{3,2,1,0:T(8,128)(2,1)S(1)} collective-permute-done((bf16[1,1,16,2048]{3,2,1,0:T(8,128)(2,1)S(1)}, bf16[1,1,16,2048]{3,2,1,0:T(8,128)(2,1)S(1)}, u32[]{:S(2)}, u32[]{:S(2)}) %collective-permute-start.3) | collective-permute-done | bytes 65568 | tf_op jit(solution)/shard_map/ppermute | solution.py:17
  75.4 0.2 concatenate.16
  75.6 6.6 %collective-permute-done.2 = bf16[1,1,16,2048]{3,2,1,0:T(8,128)(2,1)S(1)} collective-permute-done((bf16[1,1,16,2048]{3,2,1,0:T(8,128)(2,1)S(1)}, bf16[1,1,16,2048]{3,2,1,0:T(8,128)(2,1)S(1)}, u32[]{:S(2)}, u32[]{:S(2)}) %collective-permute-start.2) | collective-permute-done | bytes 65568 | tf_op jit(solution)/shard_map/ppermute | solution.py:14
  82.2 0.2 concatenate.14
  82.4 0.1 maximum_bitcast_fusion
  82.5 0.2 copy.65
  82.6 0.1 pad.4.clone
  82.7 0.1 copy.49
  82.9 0.1 slice.8
  82.9 0.1 reduce_sum.21
  83.1 0.2 reshape.104
  83.2 0.7 copy.60
  83.9 18.8 %all-to-all-start.1 = ((bf16[64,27,4]{1,2,0:T(4,128)(2,1)}), bf16[64,27,4]{1,2,0:T(4,128)(2,1)S(1)}, u32[]{:S(2)}, u32[]{:S(2)}) async-start(bf16[64,27,4]{1,2,0:T(4,128)(2,1)} %copy.60), calls=%async_computation.1 | async-start | bytes 131072 | tf_op jit(solution)/shard_map/all_to_all | solution.py:30
  102.7 1.3 %fusion.3 = bf16[1,16,8,5,64]{4,2,3,1,0:T(8,128)(2,1)S(1)} fusion(bf16[3,3,3,64,64]{4,3,2,1,0:T(8,128)(2,1)S(1)} %bitcast.64, bf16[3,16,1,7,2,64]{5,3,4,1,0,2:T(8,128)(2,1)S(1)} %slice.8, bf16[3,16,1,8,5,64]{5,3,4,1,0,2:T(8,128)(2,1)S(1)} %copy.49, pred[8,5]{0,1:T(8,128)(4,1)S(1)} %copy-done.2), kind=kOutput, calls=%fused_computation.7 | convolution fusion | flops 136773632 | bytes 634920 | tf_op jit(solution)/shard_map/conv_general_dilated | solution.py:71
  104.1 0.8 reshape.103
  104.9 10.6 %all-to-all-done.1 = bf16[64,27,4]{1,2,0:T(4,128)(2,1)S(1)} async-done(((bf16[64,27,4]{1,2,0:T(4,128)(2,1)}), bf16[64,27,4]{1,2,0:T(4,128)(2,1)S(1)}, u32[]{:S(2)}, u32[]{:S(2)}) %all-to-all-start.1) | async-done | bytes 13856 | tf_op jit(solution)/shard_map/all_to_all | solution.py:30
  115.5 0.7 convert_reduce_fusion
  (12 shorter events, 0.2 us)
Async XLA Ops:
  0.6 23.4 %copy-start.1 = (bf16[1,1,16,2048]{3,2,1,0:T(8,128)(2,1)S(1)}, bf16[1,1,16,2048]{3,2,1,0:T(8,128)(2,1)}, u32[]{:S(2)}) copy-start(bf16[1,1,16,2048]{3,2,1,0:T(8,128)(2,1)} %param.3) | copy-start | bytes 196612
  0.6 23.4 %collective-permute-start = (bf16[1,1,16,2048]{3,2,1,0:T(8,128)(2,1)}, bf16[1,1,16,2048]{3,2,1,0:T(8,128)(2,1)S(1)}, u32[]{:S(2)}, u32[]{:S(2)}) collective-permute-start(bf16[1,1,16,2048]{3,2,1,0:T(8,128)(2,1)} %param.3), channel_id=1, source_target_pairs={{0,64},{64,128},{128,192},{192,256},{256,320},{320,384},{384,448},... | collective-permute-start | bytes 196616 | tf_op jit(solution)/shard_map/ppermute | solution.py:14
  19.9 17.2 %collective-permute-start.1 = (bf16[1,1,16,2048]{3,2,1,0:T(8,128)(2,1)}, bf16[1,1,16,2048]{3,2,1,0:T(8,128)(2,1)S(1)}, u32[]{:S(2)}, u32[]{:S(2)}) collective-permute-start(bf16[1,1,16,2048]{3,2,1,0:T(8,128)(2,1)} %param.3), channel_id=1, source_target_pairs={{64,0},{128,64},{192,128},{256,192},{320,256},{384,320},{448,384},... | collective-permute-start | bytes 196616 | tf_op jit(solution)/shard_map/ppermute | solution.py:17
  38.2 0.7 copy-start.2
  45.9 37.0 %all-to-all-start = ((bf16[16,1728,4]{1,2,0:T(4,128)(2,1)}), bf16[16,1728,4]{1,2,0:T(4,128)(2,1)S(1)}, u32[]{:S(2)}, u32[]{:S(2)}) async-start(bf16[16,1728,4]{1,2,0:T(4,128)(2,1)} %bitcast.12), calls=%async_computation | async-start | bytes 458752 | tf_op jit(solution)/shard_map/all_to_all | solution.py:30
  52.7 0.8 copy-start
  54.2 21.2 %collective-permute-start.3 = (bf16[1,1,16,2048]{3,2,1,0:T(8,128)(2,1)S(1)}, bf16[1,1,16,2048]{3,2,1,0:T(8,128)(2,1)S(1)}, u32[]{:S(2)}, u32[]{:S(2)}) collective-permute-start(bf16[1,1,16,2048]{3,2,1,0:T(8,128)(2,1)S(1)} %get-tuple-element.5), channel_id=1, source_target_pairs={{64,0},{128,64},{192,128},{256,192},{320,256},{384,320},{448,384},... | collective-permute-start | bytes 196616 | tf_op jit(solution)/shard_map/ppermute | solution.py:17
  66.0 16.2 %collective-permute-start.2 = (bf16[1,1,16,2048]{3,2,1,0:T(8,128)(2,1)S(1)}, bf16[1,1,16,2048]{3,2,1,0:T(8,128)(2,1)S(1)}, u32[]{:S(2)}, u32[]{:S(2)}) collective-permute-start(bf16[1,1,16,2048]{3,2,1,0:T(8,128)(2,1)S(1)} %get-tuple-element.5), channel_id=1, source_target_pairs={{0,64},{64,128},{128,192},{192,256},{256,320},{320,384},{384,448},... | collective-permute-start | bytes 196616 | tf_op jit(solution)/shard_map/ppermute | solution.py:14
  83.9 31.6 %all-to-all-start.1 = ((bf16[64,27,4]{1,2,0:T(4,128)(2,1)}), bf16[64,27,4]{1,2,0:T(4,128)(2,1)S(1)}, u32[]{:S(2)}, u32[]{:S(2)}) async-start(bf16[64,27,4]{1,2,0:T(4,128)(2,1)} %copy.60), calls=%async_computation.1 | async-start | bytes 131072 | tf_op jit(solution)/shard_map/all_to_all | solution.py:30
